TPU v7x, 256 devices: a whole 4x4x8 slice. The times are simulated.
256 devices in a mesh: row: 16 (over z, core), col: 16 (over y, x).
Axes of the slice: x: 4, y: 4, z: 8, core: 2. Of those that a mesh axis runs over, the one named last changes fastest.
Arguments:
- matrix: bfloat16 [4096, 262144], P('row', 'col'), may hold values from -60 to 60
- test_matrix: bfloat16 [262144, 512], P(('col', 'row')), may hold values from -0.0390625 to 0.0390625
Outputs:
- orthonormal: float32 [4096, 512], P(('row', 'col'))
- triangular: float32 [512, 512], replicated
All inputs are finite; a program needn't handle non-finite values.
Results may differ from a plain program's by a relative error of at most 0.0003.
Values may be sent and summed in bfloat16 or wider, within the bound.
No kernel may reach another device: no remote copies, remote signals or barrier semaphores. Data moves between devices by JAX's collectives and lax.ppermute only.
A program may use at most 128 MiB of HBM per device.

v0:
```python
import jax
import jax.numpy as jnp
from jax import lax
from jax.sharding import PartitionSpec as P


def probe_product(matrix, test_matrix):
    return jnp.dot(
        matrix,
        lax.all_gather(test_matrix, "row", axis=0, tiled=True),
        preferred_element_type=jnp.float32,
    )


def gram_term(own_rows):
    return jnp.dot(own_rows.T, own_rows, precision=lax.Precision.HIGHEST)


def shards(matrix, test_matrix):
    share_rows = matrix.shape[0] // lax.axis_size("col")
    total_rows = matrix.shape[0] * lax.axis_size("row")
    partial_value = probe_product(matrix, test_matrix)
    sketch = lax.psum(partial_value, "col")
    gram = lax.psum(gram_term(sketch), "row")
    own_rows = lax.dynamic_slice_in_dim(sketch, lax.axis_index("col") * share_rows, share_rows, 0)
    gram = gram / jnp.float32(total_rows)
    lower_factor = jnp.linalg.cholesky(gram)
    orthonormal = lax.linalg.triangular_solve(
        lower_factor, own_rows, left_side=False, lower=True, transpose_a=True
    )
    return (orthonormal, lower_factor.T)


def solution(mesh):
    in_specs = (P("row", "col"), P(("col", "row"), None))
    out_specs = (P(("row", "col"), None), P())
    return jax.shard_map(shards, mesh=mesh, in_specs=in_specs, out_specs=out_specs, check_vma=False)
```

profile of v0, /device:TPU:2, one launch (start us, length us, event | category | flops | bytes accessed | tf_op | source)
XLA Modules:
  0.0 478.1 jit_solution(10044351522613762331)
XLA Ops:
  7.2 0.7 all-gather.2.cloned.1.call-update
  7.9 100.2 %all-gather.2.cloned.1.call-done = bf16[16384,512]{1,0:T(8,128)(2,1)} async-done(((bf16[1024,512]{1,0:T(8,128)(2,1)}), bf16[16384,512]{1,0:T(8,128)(2,1)}) %all-gather.2.cloned.1.call-update) | async-done | bytes 16777232 | tf_op jit(solution)/shard_map/all_gather | solution.py:10
  108.1 13.4 %fusion.34 = f32[256,512]{1,0:T(8,128)} fusion(bf16[256,16384]{1,0:T(8,128)(2,1)} %param.2, bf16[16384,512]{1,0:T(8,128)(2,1)} %all-gather.2.cloned.1.call-done), kind=kOutput, calls=%fused_computation.71 | convolution fusion | flops 4294967296 | bytes 25690112 | tf_op jit(solution)/shard_map/dot_general | solution.py:8
  121.6 0.2 all-reduce.6.cloned.1.call-start
  121.8 93.8 %all-reduce.4.cloned.1.call-done = f32[256,512]{1,0:T(8,128)} async-done(((f32[256,512]{1,0:T(8,128)}), f32[256,512]{1,0:T(8,128)}) %all-reduce.4.cloned.1.call-update) | async-done | bytes 524304 | tf_op jit(solution)/shard_map/psum | solution.py:23
  215.6 3.2 fusion.35
  218.9 112.2 %all-reduce.6.cloned.1.call-done = f32[512,512]{0,1:T(8,128)} async-done(((f32[512,512]{0,1:T(8,128)}), f32[512,512]{0,1:T(8,128)}) %all-reduce.6.cloned.1.call-update) | async-done | bytes 1048592 | tf_op jit(solution)/shard_map/psum | solution.py:24
  331.1 1.3 broadcast_multiply_fusion
  332.4 0.3 copy.5
  332.7 1.5 fusion
  334.2 11.7 %cholesky.104 = f32[128,128]{1,0:T(8,128)S(1)} custom-call(f32[128,128]{1,0:T(8,128)S(1)} %cholesky.266), custom_call_target="Cholesky" | custom-call | tf_op jit(solution)/shard_map/jit(cholesky)/cholesky | solution.py:27
  346.0 9.8 %custom-call.30 = f32[1,128,128]{1,2,0:T(8,128)S(1)} custom-call(f32[1,128,128]{2,1,0:T(8,128)S(1)} %get-tuple-element.33), custom_call_target="InvertDiagBlocksLowerTriangular" | custom-call | tf_op jit(solution)/shard_map/jit(cholesky)/cholesky | solution.py:27
  355.8 0.1 cholesky.224
  355.9 0.3 constant_dynamic-update-slice_fusion.2
  356.2 0.3 convolution_subtract_fusion
  356.6 11.8 %cholesky.217 = f32[128,128]{1,0:T(8,128)S(1)} custom-call(f32[128,128]{1,0:T(8,128)S(1)} %cholesky.270), custom_call_target="Cholesky" | custom-call | tf_op jit(solution)/shard_map/jit(cholesky)/cholesky | solution.py:27
  368.5 9.8 %custom-call.31 = f32[1,128,128]{1,2,0:T(8,128)S(1)} custom-call(f32[1,128,128]{2,1,0:T(8,128)S(1)} %get-tuple-element.30), custom_call_target="InvertDiagBlocksLowerTriangular" | custom-call | tf_op jit(solution)/shard_map/jit(cholesky)/cholesky | solution.py:27
  378.3 0.3 convolution_dynamic-update-slice_fusion
  378.5 0.4 convolution_subtract_fusion.1
  378.9 11.7 %cholesky.238 = f32[128,128]{1,0:T(8,128)S(1)} custom-call(f32[128,128]{1,0:T(8,128)S(1)} %cholesky.275), custom_call_target="Cholesky" | custom-call | tf_op jit(solution)/shard_map/jit(cholesky)/cholesky | solution.py:27
  390.7 0.7 compare_reduce_fusion.1
  391.4 9.8 %custom-call.32 = f32[1,128,128]{1,2,0:T(8,128)S(1)} custom-call(f32[1,128,128]{2,1,0:T(8,128)S(1)} %get-tuple-element.27), custom_call_target="InvertDiagBlocksLowerTriangular" | custom-call | tf_op jit(solution)/shard_map/jit(cholesky)/cholesky | solution.py:27
  401.2 0.2 convolution_dynamic-update-slice_fusion.1
  401.4 0.4 convolution_subtract_fusion.2
  401.8 12.0 %cholesky.255 = f32[128,128]{1,0:T(8,128)S(1)} custom-call(f32[128,128]{1,0:T(8,128)S(1)} %convolution_subtract_fusion.2), custom_call_target="Cholesky" | custom-call | tf_op jit(solution)/shard_map/jit(cholesky)/cholesky | solution.py:27
  413.8 0.6 compare_reduce_fusion
  414.5 0.7 compare_reduce_fusion.2
  417.7 0.3 fusion.2
  417.9 1.3 copy.6
  419.2 8.1 %while.1 = (s32[]{:T(128)}, f32[512,512]{1,0:T(8,128)S(1)}, s32[4,2]{0,1:T(2,128)S(1)}, f32[4,128,128]{2,1,0:T(8,128)S(1)}, s32[]{:T(128)}) while((s32[]{:T(128)}, f32[512,512]{1,0:T(8,128)S(1)}, s32[4,2]{0,1:T(2,128)S(1)}, f32[4,128,128]{2,1,0:T(8,128)S(1)}, s32[]{:T(128)}) %tuple.33), condition=%wide.while_cond, body=%wide.while_body.sunk | while | flops 2 | bytes 131181 | solution.py:28
  419.2 0.1 constant_dynamic-slice_fusion.2
  419.3 0.6 fusion.46
  419.9 1.3 bitcast_dynamic-update-slice_fusion.2
  421.3 0.6 fusion.46
  421.9 1.3 bitcast_dynamic-update-slice_fusion.2
  423.4 0.6 fusion.46
  424.0 1.3 bitcast_dynamic-update-slice_fusion.2
  425.4 0.6 fusion.46
  426.0 1.3 bitcast_dynamic-update-slice_fusion.2
  427.4 39.3 %custom-call.33 = f32[4,128,128]{1,2,0:T(8,128)S(1)} custom-call(f32[4,128,128]{2,1,0:T(8,128)S(1)} %get-tuple-element.9), custom_call_target="InvertDiagBlocksLowerTriangular" | custom-call | tf_op jit(solution)/shard_map/triangular_solve | solution.py:28
  466.7 0.9 fusion.15
  467.6 0.9 convolution_subtract_fusion.5
  468.4 0.2 fusion.13
  468.6 0.9 convolution_subtract_fusion.4
  469.6 0.2 fusion.12
  469.7 1.0 convolution_subtract_fusion.3
  470.8 0.2 fusion.11
  470.9 0.6 pad_maximum_fusion
  (17 shorter events, 0.5 us)
Async XLA Ops:
  7.2 101.0 %all-gather.2.cloned.1.call-start = ((), (), s32[]{:S(2)}) async-start(), calls=%async_computation | async-start | bytes 17825792 | tf_op jit(solution)/shard_map/all_gather | solution.py:10
  7.9 207.7 %all-reduce.4.cloned.1.call-start = ((), (), s32[]{:S(2)}) async-start(), calls=%async_computation.1 | async-start | bytes 1048576 | tf_op jit(solution)/shard_map/psum | solution.py:23
  121.6 209.5 %all-reduce.6.cloned.1.call-start = ((), (), s32[]{:S(2)}) async-start(), calls=%async_computation.2 | async-start | bytes 2097152 | tf_op jit(solution)/shard_map/psum | solution.py:24
Sparse Core Ops, SparseCore 0:
  9.8 98.2 all-gather.1
  121.7 93.8 all-reduce.3
  219.0 112.0 all-reduce.5
where the time goes:
time: 479 us; the launch traced here: 478 us
  waiting for transfers between devices  307 us (64%)
  other arithmetic  122 us (25%)
  matrix products  22.8 us (5%)
  between operations  16.5 us (3%)
  local copies, waits for them, and re-layouts  9.84 us (2%)
    psum x1, waiting for transfers between devices, shards(): gram = lax.psum(gram_term(sketch), 'row')  112 us
    all_gather x1, waiting for transfers between devices, probe_product(): lax.all_gather(test_matrix, 'row', axis=0, tiled=True)  100 us
    psum x1, waiting for transfers between devices, shards(): sketch = lax.psum(partial_value, 'col')  93.8 us
    another operation x14, other arithmetic, shards(): lower_factor = jnp.linalg.cholesky(gram)  78.8 us
    another operation x3, other arithmetic, shards(): lax.linalg.triangular_solve(lower_factor, own_rows, left_side=False, lowe...  40 us
    dot_general x1, matrix products, probe_product(): jnp.dot(matrix, lax.all_gather(test_matrix, 'row', axis=0, tiled=True), p...  13.4 us
  transfers between devices with their start and end apart: 3, of which 3 were waited for; matrix products, arithmetic and copies ran while one was open for 0% of the time, Pallas kernels for 0%

commit v1 on v0

--- a/solution.py
+++ b/solution.py
@@ -12,18 +12,32 @@
     )
 
 
-def gram_term(own_rows):
-    return jnp.dot(own_rows.T, own_rows, precision=lax.Precision.HIGHEST)
+def scatter_sum(value, axis, parts):
+    pieces = value.reshape(parts, value.shape[0] // parts, *value.shape[1:])
+    return lax.all_to_all(pieces, axis, 0, 0, tiled=False).sum(0)
+
+
+def gather_rows(value, axis, parts):
+    copies = jnp.broadcast_to(value[None], (parts, *value.shape))
+    gathered = lax.all_to_all(copies, axis, 0, 0, tiled=False)
+    return gathered.reshape(parts * value.shape[0], *value.shape[1:])
 
 
 def shards(matrix, test_matrix):
-    share_rows = matrix.shape[0] // lax.axis_size("col")
-    total_rows = matrix.shape[0] * lax.axis_size("row")
+    n_col = lax.axis_size("col")
+    n_row = lax.axis_size("row")
+    total_rows = matrix.shape[0] * n_row
+    k = test_matrix.shape[1]
     partial_value = probe_product(matrix, test_matrix)
-    sketch = lax.psum(partial_value, "col")
-    gram = lax.psum(gram_term(sketch), "row")
-    own_rows = lax.dynamic_slice_in_dim(sketch, lax.axis_index("col") * share_rows, share_rows, 0)
-    gram = gram / jnp.float32(total_rows)
+    own_rows = scatter_sum(partial_value, "col", n_col)
+    sketch = gather_rows(own_rows, "col", n_col)
+    width = k // n_col
+    col = lax.axis_index("col")
+    columns = lax.dynamic_slice_in_dim(sketch, col * width, width, 1)
+    gram_part = jnp.dot(sketch.T, columns, precision=lax.Precision.HIGHEST)
+    gram_part = gather_rows(scatter_sum(gram_part, "row", n_row), "row", n_row)
+    blocks = gather_rows(gram_part.T, "col", n_col)
+    gram = blocks.T / jnp.float32(total_rows)
     lower_factor = jnp.linalg.cholesky(gram)
     orthonormal = lax.linalg.triangular_solve(
         lower_factor, own_rows, left_side=False, lower=True, transpose_a=True

time: 479 us -> 346 us (0.72)
  waiting for transfers between devices: 307 us -> 127 us
  blocking collectives: 0 us -> 40 us
  starting transfers between devices: 0.3 us -> 9.72 us
  matrix products: 22.8 us -> 14.5 us
    psum x2 -> x0, waiting for transfers between devices: 206 us -> none  [the longest x1 112 us: shards(): gram = lax.psum(gram_term(sketch), 'row')]
    all_to_all x0 -> x3, blocking collectives: none -> 40 us  [the longest x2 29.6 us: scatter_sum(): return lax.all_to_all(pieces, axis, 0, 0, tiled=False).sum(0)]
    all_to_all x0 -> x2, waiting for transfers between devices: none -> 26.3 us  [gather_rows(): gathered = lax.all_to_all(copies, axis, 0, 0, tiled=False)]
    all_to_all x0 -> x2, starting transfers between devices: none -> 9.68 us  [gather_rows(): gathered = lax.all_to_all(copies, axis, 0, 0, tiled=False)]
where the time goes in v1:
time: 346 us; the launch traced here: 343 us
  waiting for transfers between devices  127 us (37%)
  other arithmetic  121 us (35%)
  blocking collectives  40 us (12%)
  between operations  16.8 us (5%)
  matrix products  14.5 us (4%)
  local copies, waits for them, and re-layouts  13.8 us (4%)
  starting transfers between devices  9.72 us (3%)
    all_gather x1, waiting for transfers between devices, probe_product(): lax.all_gather(test_matrix, 'row', axis=0, tiled=True)  100 us
    another operation x14, other arithmetic, shards(): lower_factor = jnp.linalg.cholesky(gram)  78.6 us
    another operation x3, other arithmetic, shards(): lax.linalg.triangular_solve(lower_factor, own_rows, left_side=False, lowe...  40 us
    all_to_all x2, blocking collectives, scatter_sum(): return lax.all_to_all(pieces, axis, 0, 0, tiled=False).sum(0)  29.6 us
    all_to_all x2, waiting for transfers between devices, gather_rows(): gathered = lax.all_to_all(copies, axis, 0, 0, tiled=False)  26.3 us
    dot_general x1, matrix products, probe_product(): jnp.dot(matrix, lax.all_gather(test_matrix, 'row', axis=0, tiled=True), p...  10.5 us
    all_to_all x1, blocking collectives, gather_rows(): gathered = lax.all_to_all(copies, axis, 0, 0, tiled=False)  10.4 us
    all_to_all x2, starting transfers between devices, gather_rows(): gathered = lax.all_to_all(copies, axis, 0, 0, tiled=False)  9.68 us
  transfers between devices with their start and end apart: 3, of which 3 were waited for; matrix products, arithmetic and copies ran while one was open for 0% of the time, Pallas kernels for 0%

profile of v1, /device:TPU:2, one launch (start us, length us, event | category | flops | bytes accessed | tf_op | source)
XLA Modules:
  0.0 343.1 jit_solution(3495870859918004758)
XLA Ops:
  7.2 0.7 all-gather.2.cloned.1.call-update
  7.9 100.2 %all-gather.2.cloned.1.call-done = bf16[16384,512]{1,0:T(8,128)(2,1)} async-done(((bf16[1024,512]{1,0:T(8,128)(2,1)}), bf16[16384,512]{1,0:T(8,128)(2,1)}) %all-gather.2.cloned.1.call-update) | async-done | bytes 16777232 | tf_op jit(solution)/shard_map/all_gather | solution.py:10
  108.1 10.5 %fusion.37 = f32[256,512]{1,0:T(8,128)S(1)} fusion(bf16[256,16384]{1,0:T(8,128)(2,1)} %param.2, bf16[16384,512]{1,0:T(8,128)(2,1)} %all-gather.2.cloned.1.call-done), kind=kOutput, calls=%fused_computation.74 | convolution fusion | flops 4294967296 | bytes 25690112 | tf_op jit(solution)/shard_map/dot_general | solution.py:8
  118.6 17.7 %all_to_all.25 = f32[16,16,512]{2,1,0:T(8,128)S(1)} all-to-all(f32[16,16,512]{2,1,0:T(8,128)S(1)} %bitcast.75), channel_id=1, replica_groups=mesh['row'=16,'col'=16] {'col'}, dimensions={0} | all-to-all | bytes 1048576 | tf_op jit(solution)/shard_map/all_to_all | solution.py:17
  136.3 0.9 broadcast_in_dim.7
  137.2 4.8 %all-to-all-start.1 = ((f32[16,16,512]{2,1,0:T(8,128)}), f32[16,16,512]{2,1,0:T(8,128)S(1)}, u32[]{:S(2)}, u32[]{:S(2)}) async-start(f32[16,16,512]{2,1,0:T(8,128)} %broadcast_in_dim.7), calls=%async_computation.1 | async-start | bytes 1048576 | tf_op jit(solution)/shard_map/all_to_all | solution.py:22
  142.0 9.6 %all-to-all-done.1 = f32[16,16,512]{2,1,0:T(8,128)S(1)} async-done(((f32[16,16,512]{2,1,0:T(8,128)}), f32[16,16,512]{2,1,0:T(8,128)S(1)}, u32[]{:S(2)}, u32[]{:S(2)}) %all-to-all-start.1) | async-done | bytes 524320 | tf_op jit(solution)/shard_map/all_to_all | solution.py:22
  151.8 0.7 fusion.11
  152.7 12.0 %all_to_all.26 = f32[16,1,1024]{2,1,0:T(1,128)S(1)} all-to-all(f32[16,1,1024]{2,1,0:T(1,128)S(1)} %reshape.80), channel_id=1, replica_groups=mesh['row'=16,'col'=16] {'row'}, dimensions={0} | all-to-all | bytes 131072 | tf_op jit(solution)/shard_map/all_to_all | solution.py:17
  164.6 0.5 broadcast.197
  165.1 0.8 reduce.24
  166.4 10.4 %all_to_all.27 = f32[16,1,1024]{2,1,0:T(1,128)S(1)} all-to-all(f32[16,1,1024]{2,1,0:T(1,128)S(1)} %reshape.82), channel_id=1, replica_groups=mesh['row'=16,'col'=16] {'row'}, dimensions={0} | all-to-all | bytes 131072 | tf_op jit(solution)/shard_map/all_to_all | solution.py:22
  176.7 0.8 reduce.25
  178.0 1.1 broadcast_in_dim.9
  179.1 4.9 %all-to-all-start.4 = ((f32[16,32,512]{2,1,0:T(8,128)}), f32[16,32,512]{2,1,0:T(8,128)S(1)}, u32[]{:S(2)}, u32[]{:S(2)}) async-start(f32[16,32,512]{2,1,0:T(8,128)} %broadcast_in_dim.9), calls=%async_computation.4 | async-start | bytes 2097152 | tf_op jit(solution)/shard_map/all_to_all | solution.py:22
  183.9 16.7 %all-to-all-done.4 = f32[16,32,512]{2,1,0:T(8,128)S(1)} async-done(((f32[16,32,512]{2,1,0:T(8,128)}), f32[16,32,512]{2,1,0:T(8,128)S(1)}, u32[]{:S(2)}, u32[]{:S(2)}) %all-to-all-start.4) | async-done | bytes 1048608 | tf_op jit(solution)/shard_map/all_to_all | solution.py:22
  200.6 0.3 copy.19
  201.0 0.2 fusion
  201.2 11.7 %cholesky.104 = f32[128,128]{1,0:T(8,128)S(1)} custom-call(f32[128,128]{1,0:T(8,128)S(1)} %cholesky.266), custom_call_target="Cholesky" | custom-call | tf_op jit(solution)/shard_map/jit(cholesky)/cholesky | solution.py:41
  213.1 9.8 %custom-call.30 = f32[1,128,128]{1,2,0:T(8,128)S(1)} custom-call(f32[1,128,128]{2,1,0:T(8,128)S(1)} %get-tuple-element.39), custom_call_target="InvertDiagBlocksLowerTriangular" | custom-call | tf_op jit(solution)/shard_map/jit(cholesky)/cholesky | solution.py:41
  222.9 0.3 constant_dynamic-update-slice_fusion.3
  223.2 0.3 convolution_subtract_fusion
  223.6 11.7 %cholesky.217 = f32[128,128]{1,0:T(8,128)S(1)} custom-call(f32[128,128]{1,0:T(8,128)S(1)} %cholesky.270), custom_call_target="Cholesky" | custom-call | tf_op jit(solution)/shard_map/jit(cholesky)/cholesky | solution.py:41
  235.4 10.0 %custom-call.31 = f32[1,128,128]{1,2,0:T(8,128)S(1)} custom-call(f32[1,128,128]{2,1,0:T(8,128)S(1)} %get-tuple-element.36), custom_call_target="InvertDiagBlocksLowerTriangular" | custom-call | tf_op jit(solution)/shard_map/jit(cholesky)/cholesky | solution.py:41
  245.3 0.3 convolution_dynamic-update-slice_fusion
  245.6 0.4 convolution_subtract_fusion.1
  246.0 11.7 %cholesky.238 = f32[128,128]{1,0:T(8,128)S(1)} custom-call(f32[128,128]{1,0:T(8,128)S(1)} %cholesky.275), custom_call_target="Cholesky" | custom-call | tf_op jit(solution)/shard_map/jit(cholesky)/cholesky | solution.py:41
  257.8 9.8 %custom-call.32 = f32[1,128,128]{1,2,0:T(8,128)S(1)} custom-call(f32[1,128,128]{2,1,0:T(8,128)S(1)} %get-tuple-element.33), custom_call_target="InvertDiagBlocksLowerTriangular" | custom-call | tf_op jit(solution)/shard_map/jit(cholesky)/cholesky | solution.py:41
  267.6 0.2 convolution_dynamic-update-slice_fusion.1
  267.8 0.4 convolution_subtract_fusion.2
  268.2 11.7 %cholesky.255 = f32[128,128]{1,0:T(8,128)S(1)} custom-call(f32[128,128]{1,0:T(8,128)S(1)} %convolution_subtract_fusion.2), custom_call_target="Cholesky" | custom-call | tf_op jit(solution)/shard_map/jit(cholesky)/cholesky | solution.py:41
  279.9 0.7 compare_reduce_fusion.1
  280.7 0.6 compare_reduce_fusion
  281.3 0.7 compare_reduce_fusion.2
  284.5 0.5 fusion.2
  285.0 8.5 %while.1 = (s32[]{:T(128)}, f32[512,512]{1,0:T(8,128)S(1)}, s32[4,2]{0,1:T(2,128)S(1)}, f32[4,128,128]{2,1,0:T(8,128)S(1)}, s32[]{:T(128)}) while((s32[]{:T(128)}, f32[512,512]{1,0:T(8,128)S(1)}, s32[4,2]{0,1:T(2,128)S(1)}, f32[4,128,128]{2,1,0:T(8,128)S(1)}, s32[]{:T(128)}) %tuple.36), condition=%wide.while_cond, body=%wide.while_body.sunk | while | flops 2 | bytes 131189 | solution.py:42
  285.1 0.6 fusion.47
  285.7 1.4 bitcast_dynamic-update-slice_fusion.2
  287.2 0.6 fusion.47
  287.8 1.4 bitcast_dynamic-update-slice_fusion.2
  289.3 0.6 fusion.47
  289.9 1.4 bitcast_dynamic-update-slice_fusion.2
  291.5 0.6 fusion.47
  292.0 1.4 bitcast_dynamic-update-slice_fusion.2
  293.5 39.3 %custom-call.33 = f32[4,128,128]{1,2,0:T(8,128)S(1)} custom-call(f32[4,128,128]{2,1,0:T(8,128)S(1)} %get-tuple-element.9), custom_call_target="InvertDiagBlocksLowerTriangular" | custom-call | tf_op jit(solution)/shard_map/triangular_solve | solution.py:42
  333.8 0.3 convolution_subtract_fusion.3
  334.3 0.6 pad_maximum_fusion
  334.9 1.3 copy.20
  (33 shorter events, 3.0 us)
Async XLA Ops:
  7.2 101.0 %all-gather.2.cloned.1.call-start = ((), (), s32[]{:S(2)}) async-start(), calls=%async_computation.5 | async-start | bytes 17825792 | tf_op jit(solution)/shard_map/all_gather | solution.py:10
  137.2 14.4 %all-to-all-start.1 = ((f32[16,16,512]{2,1,0:T(8,128)}), f32[16,16,512]{2,1,0:T(8,128)S(1)}, u32[]{:S(2)}, u32[]{:S(2)}) async-start(f32[16,16,512]{2,1,0:T(8,128)} %broadcast_in_dim.7), calls=%async_computation.1 | async-start | bytes 1048576 | tf_op jit(solution)/shard_map/all_to_all | solution.py:22
  179.1 21.6 %all-to-all-start.4 = ((f32[16,32,512]{2,1,0:T(8,128)}), f32[16,32,512]{2,1,0:T(8,128)S(1)}, u32[]{:S(2)}, u32[]{:S(2)}) async-start(f32[16,32,512]{2,1,0:T(8,128)} %broadcast_in_dim.9), calls=%async_computation.4 | async-start | bytes 2097152 | tf_op jit(solution)/shard_map/all_to_all | solution.py:22
Sparse Core Ops, SparseCore 0:
  9.8 98.2 all-gather.1

commit v2 on v1

--- a/solution.py
+++ b/solution.py
@@ -1,7 +1,53 @@
 import jax
 import jax.numpy as jnp
 from jax import lax
+from jax.experimental import pallas as pl
+from jax.experimental.pallas import tpu as pltpu
 from jax.sharding import PartitionSpec as P
+
+PANEL = 128
+
+
+def factor_kernel(a_ref, r_ref, w_ref):
+    n, width = a_ref.shape
+    w_ref[...] = a_ref[...]
+    for k in range(n // PANEL):
+        base = k * PANEL
+        lanes = lax.broadcasted_iota(jnp.int32, (1, width - base), 1) + base
+        if base:
+            r_ref[base:base + PANEL, :base] = jnp.zeros((PANEL, base), jnp.float32)
+
+        def step(t, carry, base=base, lanes=lanes):
+            j = base + t
+            row = w_ref[pl.ds(j, 1), base:]
+            pivot = jnp.sum(jnp.where(lanes == j, row, 0.0), axis=1, keepdims=True)
+            scale = lax.rsqrt(pivot)
+            scale = scale * (1.5 - 0.5 * pivot * scale * scale)
+            top = jnp.where(lanes >= j, row * scale, 0.0)
+            r_ref[pl.ds(j, 1), base:] = top
+            head = jnp.broadcast_to(top[:, :PANEL], (8, PANEL))
+            column = jnp.transpose(head)[:, 0:1]
+            w_ref[base:base + PANEL, base:] = w_ref[base:base + PANEL, base:] - column * top
+            return carry
+
+        lax.fori_loop(0, PANEL, step, 0)
+        rest = base + PANEL
+        if rest < n:
+            block = r_ref[base:rest, rest:]
+            left = jnp.transpose(block[:, :n - rest])
+            update = jnp.dot(left, block, precision=lax.Precision.HIGHEST, preferred_element_type=jnp.float32)
+            w_ref[rest:n, rest:] = w_ref[rest:n, rest:] - update
+
+
+def factor(augmented):
+    n, width = augmented.shape
+    return pl.pallas_call(
+        factor_kernel,
+        out_shape=jax.ShapeDtypeStruct((n, width), jnp.float32),
+        in_specs=[pl.BlockSpec(memory_space=pltpu.VMEM)],
+        out_specs=pl.BlockSpec(memory_space=pltpu.VMEM),
+        scratch_shapes=[pltpu.VMEM((n, width), jnp.float32)],
+    )(augmented)
 
 
 def probe_product(matrix, test_matrix):
@@ -38,11 +84,10 @@
     gram_part = gather_rows(scatter_sum(gram_part, "row", n_row), "row", n_row)
     blocks = gather_rows(gram_part.T, "col", n_col)
     gram = blocks.T / jnp.float32(total_rows)
-    lower_factor = jnp.linalg.cholesky(gram)
-    orthonormal = lax.linalg.triangular_solve(
-        lower_factor, own_rows, left_side=False, lower=True, transpose_a=True
-    )
-    return (orthonormal, lower_factor.T)
+    share = own_rows.shape[0]
+    pad = jnp.zeros((k, PANEL - share), jnp.float32)
+    factored = factor(jnp.concatenate([gram, own_rows.T, pad], axis=1))
+    return (factored[:, k:k + share].T, factored[:, :k])
 
 
 def solution(mesh):

time: 346 us -> 357 us (1.032)
  Pallas kernels: 0 us -> 141 us
  other arithmetic: 121 us -> 2.97 us
  local copies, waits for them, and re-layouts: 13.8 us -> 8.08 us
    pallas_call x0 -> x1, Pallas kernels: none -> 141 us  [factor(): pl.pallas_call(factor_kernel, out_shape=jax.ShapeDtypeStruct((n, width),...]
    another operation x17 -> x0, other arithmetic: 119 us -> none  [the longest x14 78.6 us: shards(): lower_factor = jnp.linalg.cholesky(gram)]
    another operation x17 -> x0, local copies, waits for them, and re-layouts: 8.54 us -> none
where the time goes in v2:
time: 357 us; the launch traced here: 354 us
  Pallas kernels  141 us (39%)
  waiting for transfers between devices  127 us (36%)
  blocking collectives  40 us (11%)
  between operations  14.1 us (4%)
  matrix products  11.2 us (3%)
  starting transfers between devices  9.72 us (3%)
  local copies, waits for them, and re-layouts  8.08 us (2%)
    pallas_call x1, Pallas kernels, factor(): pl.pallas_call(factor_kernel, out_shape=jax.ShapeDtypeStruct((n, width),...  141 us
    all_gather x1, waiting for transfers between devices, probe_product(): lax.all_gather(test_matrix, 'row', axis=0, tiled=True)  100 us
    all_to_all x2, blocking collectives, scatter_sum(): return lax.all_to_all(pieces, axis, 0, 0, tiled=False).sum(0)  29.6 us
    all_to_all x2, waiting for transfers between devices, gather_rows(): gathered = lax.all_to_all(copies, axis, 0, 0, tiled=False)  26.1 us
    dot_general x1, matrix products, probe_product(): jnp.dot(matrix, lax.all_gather(test_matrix, 'row', axis=0, tiled=True), p...  10.5 us
    all_to_all x1, blocking collectives, gather_rows(): gathered = lax.all_to_all(copies, axis, 0, 0, tiled=False)  10.4 us
    all_to_all x2, starting transfers between devices, gather_rows(): gathered = lax.all_to_all(copies, axis, 0, 0, tiled=False)  9.68 us
  transfers between devices with their start and end apart: 3, of which 3 were waited for; matrix products, arithmetic and copies ran while one was open for 0% of the time, Pallas kernels for 0%

profile of v2, /device:TPU:2, one launch (start us, length us, event | category | flops | bytes accessed | tf_op | source)
XLA Modules:
  0.0 353.8 jit_solution(7103566177451417880)
XLA Ops:
  7.2 0.0 all-gather.2.cloned.1.call-start
  7.2 0.7 all-gather.2.cloned.1.call-update
  7.9 100.2 %all-gather.2.cloned.1.call-done = bf16[16384,512]{1,0:T(8,128)(2,1)} async-done(((bf16[1024,512]{1,0:T(8,128)(2,1)}), bf16[16384,512]{1,0:T(8,128)(2,1)}) %all-gather.2.cloned.1.call-update) | async-done | bytes 16777232 | tf_op jit(solution)/shard_map/all_gather | solution.py:56
  108.1 10.5 %fusion.4 = f32[256,512]{1,0:T(8,128)S(1)} fusion(bf16[256,16384]{1,0:T(8,128)(2,1)} %param.2, bf16[16384,512]{1,0:T(8,128)(2,1)} %all-gather.2.cloned.1.call-done), kind=kOutput, calls=%fused_computation.8 | convolution fusion | flops 4294967296 | bytes 25690112 | tf_op jit(solution)/shard_map/dot_general | solution.py:54
  118.6 17.7 %all_to_all.25 = f32[16,16,512]{2,1,0:T(8,128)S(1)} all-to-all(f32[16,16,512]{2,1,0:T(8,128)S(1)} %bitcast.30), channel_id=1, replica_groups=mesh['row'=16,'col'=16] {'col'}, dimensions={0} | all-to-all | bytes 1048576 | tf_op jit(solution)/shard_map/all_to_all | solution.py:63
  136.3 0.9 broadcast_in_dim.8
  137.2 4.8 %all-to-all-start.1 = ((f32[16,16,512]{2,1,0:T(8,128)}), f32[16,16,512]{2,1,0:T(8,128)S(1)}, u32[]{:S(2)}, u32[]{:S(2)}) async-start(f32[16,16,512]{2,1,0:T(8,128)} %broadcast_in_dim.8), calls=%async_computation.1 | async-start | bytes 1048576 | tf_op jit(solution)/shard_map/all_to_all | solution.py:68
  142.0 9.6 %all-to-all-done.1 = f32[16,16,512]{2,1,0:T(8,128)S(1)} async-done(((f32[16,16,512]{2,1,0:T(8,128)}), f32[16,16,512]{2,1,0:T(8,128)S(1)}, u32[]{:S(2)}, u32[]{:S(2)}) %all-to-all-start.1) | async-done | bytes 524320 | tf_op jit(solution)/shard_map/all_to_all | solution.py:68
  151.6 0.2 copy.16
  151.8 0.7 fusion
  152.5 0.2 reshape.25
  152.6 12.0 %all_to_all.26 = f32[16,1,1024]{2,1,0:T(1,128)S(1)} all-to-all(f32[16,1,1024]{2,1,0:T(1,128)S(1)} %reshape.25), channel_id=1, replica_groups=mesh['row'=16,'col'=16] {'row'}, dimensions={0} | all-to-all | bytes 131072 | tf_op jit(solution)/shard_map/all_to_all | solution.py:63
  164.6 0.5 broadcast.10
  165.1 0.8 reduce
  165.9 0.1 reshape.26
  166.1 0.1 copy.18
  166.2 0.2 reshape.27
  166.4 10.4 %all_to_all.27 = f32[16,1,1024]{2,1,0:T(1,128)S(1)} all-to-all(f32[16,1,1024]{2,1,0:T(1,128)S(1)} %reshape.27), channel_id=1, replica_groups=mesh['row'=16,'col'=16] {'row'}, dimensions={0} | all-to-all | bytes 131072 | tf_op jit(solution)/shard_map/all_to_all | solution.py:68
  176.7 0.8 reduce.1
  177.6 0.1 reshape.28
  177.7 0.2 copy.19
  177.8 0.1 reshape.23
  178.0 1.1 broadcast_in_dim.10
  179.1 4.9 %all-to-all-start.4 = ((f32[16,32,512]{2,1,0:T(8,128)}), f32[16,32,512]{2,1,0:T(8,128)S(1)}, u32[]{:S(2)}, u32[]{:S(2)}) async-start(f32[16,32,512]{2,1,0:T(8,128)} %broadcast_in_dim.10), calls=%async_computation.4 | async-start | bytes 2097152 | tf_op jit(solution)/shard_map/all_to_all | solution.py:68
  183.9 0.1 pad.2.clone
  184.0 0.1 copy.21
  184.1 16.5 %all-to-all-done.4 = f32[16,32,512]{2,1,0:T(8,128)S(1)} async-done(((f32[16,32,512]{2,1,0:T(8,128)}), f32[16,32,512]{2,1,0:T(8,128)S(1)}, u32[]{:S(2)}, u32[]{:S(2)}) %all-to-all-start.4) | async-done | bytes 1048608 | tf_op jit(solution)/shard_map/all_to_all | solution.py:68
  200.6 0.1 broadcast_multiply_fusion
  200.7 0.3 copy.20
  201.1 1.2 maximum_maximum_fusion.a_ref
  202.3 140.7 %shard_map.41 = f32[512,640]{1,0:T(8,128)} custom-call(f32[512,640]{1,0:T(8,128)} %maximum_maximum_fusion.a_ref), custom_call_target="tpu_custom_call" | custom-call | tf_op jit(solution)/shard_map/pallas_call | solution.py:44
  343.0 1.0 slice_bitcast_fusion
  344.0 2.3 slice.9
  346.2 0.7 copy.22
  (4 shorter events, 0.1 us)
Async XLA Ops:
  7.2 101.0 %all-gather.2.cloned.1.call-start = ((), (), s32[]{:S(2)}) async-start(), calls=%async_computation.5 | async-start | bytes 17825792 | tf_op jit(solution)/shard_map/all_gather | solution.py:56
  137.2 14.4 %all-to-all-start.1 = ((f32[16,16,512]{2,1,0:T(8,128)}), f32[16,16,512]{2,1,0:T(8,128)S(1)}, u32[]{:S(2)}, u32[]{:S(2)}) async-start(f32[16,16,512]{2,1,0:T(8,128)} %broadcast_in_dim.8), calls=%async_computation.1 | async-start | bytes 1048576 | tf_op jit(solution)/shard_map/all_to_all | solution.py:68
  179.1 21.6 %all-to-all-start.4 = ((f32[16,32,512]{2,1,0:T(8,128)}), f32[16,32,512]{2,1,0:T(8,128)S(1)}, u32[]{:S(2)}, u32[]{:S(2)}) async-start(f32[16,32,512]{2,1,0:T(8,128)} %broadcast_in_dim.10), calls=%async_computation.4 | async-start | bytes 2097152 | tf_op jit(solution)/shard_map/all_to_all | solution.py:68
Sparse Core Ops, SparseCore 0:
  9.8 98.2 all-gather.1

commit v3 on v2

--- a/solution.py
+++ b/solution.py
@@ -6,31 +6,51 @@
 from jax.sharding import PartitionSpec as P
 
 PANEL = 128
+GROUP = 8
 
 
-def factor_kernel(a_ref, r_ref, w_ref):
+def factor_kernel(a_ref, r_ref, w_ref, head_ref):
     n, width = a_ref.shape
     w_ref[...] = a_ref[...]
+    head_ref[...] = jnp.zeros(head_ref.shape, jnp.float32)
+    subl = lax.broadcasted_iota(jnp.int32, (GROUP, 1), 0)
     for k in range(n // PANEL):
         base = k * PANEL
-        lanes = lax.broadcasted_iota(jnp.int32, (1, width - base), 1) + base
+        span = width - base
+        lanes = lax.broadcasted_iota(jnp.int32, (GROUP, span), 1) + base
         if base:
             r_ref[base:base + PANEL, :base] = jnp.zeros((PANEL, base), jnp.float32)
 
-        def step(t, carry, base=base, lanes=lanes):
-            j = base + t
-            row = w_ref[pl.ds(j, 1), base:]
-            pivot = jnp.sum(jnp.where(lanes == j, row, 0.0), axis=1, keepdims=True)
-            scale = lax.rsqrt(pivot)
-            scale = scale * (1.5 - 0.5 * pivot * scale * scale)
-            top = jnp.where(lanes >= j, row * scale, 0.0)
-            r_ref[pl.ds(j, 1), base:] = top
-            head = jnp.broadcast_to(top[:, :PANEL], (8, PANEL))
-            column = jnp.transpose(head)[:, 0:1]
-            w_ref[base:base + PANEL, base:] = w_ref[base:base + PANEL, base:] - column * top
+        def group(g, carry, base=base, span=span, lanes=lanes):
+            r0 = pl.multiple_of(base + g * GROUP, GROUP)
+            block = w_ref[pl.ds(r0, GROUP), base:]
+            rows = jnp.zeros((GROUP, span), jnp.float32)
+            for t in range(GROUP):
+                j = r0 + t
+                column = jnp.sum(jnp.where(lanes[:, :PANEL] == j, block[:, :PANEL], 0.0), axis=1, keepdims=True)
+                pivot = column[t:t + 1, :]
+                scale = lax.rsqrt(pivot)
+                scale = scale * (1.5 - 0.5 * pivot * scale * scale)
+                top = jnp.where(lanes[:1] >= j, block[t:t + 1, :] * scale, 0.0)
+                rows = jnp.where(subl == t, top, rows)
+                factor_col = jnp.where(subl > t, column * scale, 0.0)
+                block = block - factor_col * top
+            r_ref[pl.ds(r0, GROUP), base:] = rows
+            head_ref[:, :GROUP] = jnp.transpose(rows[:, :PANEL])[:, :GROUP]
+
+            def slab(s, c):
+                at = pl.multiple_of(base + s * GROUP, GROUP)
+                part = w_ref[pl.ds(at, GROUP), base:]
+                mult = head_ref[pl.ds(pl.multiple_of(s * GROUP, GROUP), GROUP), :]
+                for t in range(GROUP):
+                    part = part - mult[:, t:t + 1] * rows[t:t + 1, :]
+                w_ref[pl.ds(at, GROUP), base:] = part
+                return c
+
+            lax.fori_loop(g + 1, PANEL // GROUP, slab, 0)
             return carry
 
-        lax.fori_loop(0, PANEL, step, 0)
+        lax.fori_loop(0, PANEL // GROUP, group, 0)
         rest = base + PANEL
         if rest < n:
             block = r_ref[base:rest, rest:]
@@ -46,7 +66,7 @@
         out_shape=jax.ShapeDtypeStruct((n, width), jnp.float32),
         in_specs=[pl.BlockSpec(memory_space=pltpu.VMEM)],
         out_specs=pl.BlockSpec(memory_space=pltpu.VMEM),
-        scratch_shapes=[pltpu.VMEM((n, width), jnp.float32)],
+        scratch_shapes=[pltpu.VMEM((n, width), jnp.float32), pltpu.VMEM((PANEL, PANEL), jnp.float32)],
     )(augmented)
 
 

time: 357 us -> 314 us (0.88)
  Pallas kernels: 141 us -> 97.9 us
    pallas_call x1, Pallas kernels: 141 us -> 97.9 us  [factor(): pl.pallas_call(factor_kernel, out_shape=jax.ShapeDtypeStruct((n, width),...]
where the time goes in v3:
time: 314 us; the launch traced here: 311 us
  waiting for transfers between devices  127 us (40%)
  Pallas kernels  97.9 us (31%)
  blocking collectives  40 us (13%)
  between operations  14.1 us (4%)
  matrix products  11.2 us (4%)
  starting transfers between devices  9.72 us (3%)
  local copies, waits for them, and re-layouts  8.08 us (3%)
    all_gather x1, waiting for transfers between devices, probe_product(): lax.all_gather(test_matrix, 'row', axis=0, tiled=True)  100 us
    pallas_call x1, Pallas kernels, factor(): pl.pallas_call(factor_kernel, out_shape=jax.ShapeDtypeStruct((n, width),...  97.9 us
    all_to_all x2, blocking collectives, scatter_sum(): return lax.all_to_all(pieces, axis, 0, 0, tiled=False).sum(0)  29.6 us
    all_to_all x2, waiting for transfers between devices, gather_rows(): gathered = lax.all_to_all(copies, axis, 0, 0, tiled=False)  26.1 us
    dot_general x1, matrix products, probe_product(): jnp.dot(matrix, lax.all_gather(test_matrix, 'row', axis=0, tiled=True), p...  10.5 us
    all_to_all x1, blocking collectives, gather_rows(): gathered = lax.all_to_all(copies, axis, 0, 0, tiled=False)  10.4 us
    all_to_all x2, starting transfers between devices, gather_rows(): gathered = lax.all_to_all(copies, axis, 0, 0, tiled=False)  9.68 us
  transfers between devices with their start and end apart: 3, of which 3 were waited for; matrix products, arithmetic and copies ran while one was open for 0% of the time, Pallas kernels for 0%

profile of v3, /device:TPU:2, one launch (start us, length us, event | category | flops | bytes accessed | tf_op | source)
XLA Modules:
  0.0 311.0 jit_solution(4266489944414193083)
XLA Ops:
  7.2 0.0 all-gather.2.cloned.1.call-start
  7.2 0.7 all-gather.2.cloned.1.call-update
  7.9 100.2 %all-gather.2.cloned.1.call-done = bf16[16384,512]{1,0:T(8,128)(2,1)} async-done(((bf16[1024,512]{1,0:T(8,128)(2,1)}), bf16[16384,512]{1,0:T(8,128)(2,1)}) %all-gather.2.cloned.1.call-update) | async-done | bytes 16777232 | tf_op jit(solution)/shard_map/all_gather | solution.py:76
  108.1 10.5 %fusion.4 = f32[256,512]{1,0:T(8,128)S(1)} fusion(bf16[256,16384]{1,0:T(8,128)(2,1)} %param.2, bf16[16384,512]{1,0:T(8,128)(2,1)} %all-gather.2.cloned.1.call-done), kind=kOutput, calls=%fused_computation.8 | convolution fusion | flops 4294967296 | bytes 25690112 | tf_op jit(solution)/shard_map/dot_general | solution.py:74
  118.6 17.7 %all_to_all.25 = f32[16,16,512]{2,1,0:T(8,128)S(1)} all-to-all(f32[16,16,512]{2,1,0:T(8,128)S(1)} %bitcast.30), channel_id=1, replica_groups=mesh['row'=16,'col'=16] {'col'}, dimensions={0} | all-to-all | bytes 1048576 | tf_op jit(solution)/shard_map/all_to_all | solution.py:83
  136.3 0.9 broadcast_in_dim.8
  137.2 4.8 %all-to-all-start.1 = ((f32[16,16,512]{2,1,0:T(8,128)}), f32[16,16,512]{2,1,0:T(8,128)S(1)}, u32[]{:S(2)}, u32[]{:S(2)}) async-start(f32[16,16,512]{2,1,0:T(8,128)} %broadcast_in_dim.8), calls=%async_computation.1 | async-start | bytes 1048576 | tf_op jit(solution)/shard_map/all_to_all | solution.py:88
  142.0 9.6 %all-to-all-done.1 = f32[16,16,512]{2,1,0:T(8,128)S(1)} async-done(((f32[16,16,512]{2,1,0:T(8,128)}), f32[16,16,512]{2,1,0:T(8,128)S(1)}, u32[]{:S(2)}, u32[]{:S(2)}) %all-to-all-start.1) | async-done | bytes 524320 | tf_op jit(solution)/shard_map/all_to_all | solution.py:88
  151.6 0.2 copy.16
  151.8 0.7 fusion
  152.5 0.2 reshape.25
  152.6 12.0 %all_to_all.26 = f32[16,1,1024]{2,1,0:T(1,128)S(1)} all-to-all(f32[16,1,1024]{2,1,0:T(1,128)S(1)} %reshape.25), channel_id=1, replica_groups=mesh['row'=16,'col'=16] {'row'}, dimensions={0} | all-to-all | bytes 131072 | tf_op jit(solution)/shard_map/all_to_all | solution.py:83
  164.6 0.5 broadcast.10
  165.1 0.8 reduce
  165.9 0.1 reshape.26
  166.1 0.1 copy.18
  166.2 0.2 reshape.27
  166.4 10.4 %all_to_all.27 = f32[16,1,1024]{2,1,0:T(1,128)S(1)} all-to-all(f32[16,1,1024]{2,1,0:T(1,128)S(1)} %reshape.27), channel_id=1, replica_groups=mesh['row'=16,'col'=16] {'row'}, dimensions={0} | all-to-all | bytes 131072 | tf_op jit(solution)/shard_map/all_to_all | solution.py:88
  176.7 0.8 reduce.1
  177.6 0.1 reshape.28
  177.7 0.2 copy.19
  177.8 0.1 reshape.23
  178.0 1.1 broadcast_in_dim.10
  179.1 4.9 %all-to-all-start.4 = ((f32[16,32,512]{2,1,0:T(8,128)}), f32[16,32,512]{2,1,0:T(8,128)S(1)}, u32[]{:S(2)}, u32[]{:S(2)}) async-start(f32[16,32,512]{2,1,0:T(8,128)} %broadcast_in_dim.10), calls=%async_computation.4 | async-start | bytes 2097152 | tf_op jit(solution)/shard_map/all_to_all | solution.py:88
  183.9 0.1 pad.2.clone
  184.0 0.1 copy.21
  184.1 16.5 %all-to-all-done.4 = f32[16,32,512]{2,1,0:T(8,128)S(1)} async-done(((f32[16,32,512]{2,1,0:T(8,128)}), f32[16,32,512]{2,1,0:T(8,128)S(1)}, u32[]{:S(2)}, u32[]{:S(2)}) %all-to-all-start.4) | async-done | bytes 1048608 | tf_op jit(solution)/shard_map/all_to_all | solution.py:88
  200.6 0.1 broadcast_multiply_fusion
  200.7 0.3 copy.20
  201.1 1.2 maximum_maximum_fusion.a_ref
  202.3 97.9 %shard_map.41 = f32[512,640]{1,0:T(8,128)} custom-call(f32[512,640]{1,0:T(8,128)} %maximum_maximum_fusion.a_ref), custom_call_target="tpu_custom_call" | custom-call | tf_op jit(solution)/shard_map/pallas_call | solution.py:64
  300.2 1.0 slice_bitcast_fusion
  301.1 2.3 slice.9
  303.4 0.7 copy.22
  (4 shorter events, 0.1 us)
Async XLA Ops:
  7.2 101.0 %all-gather.2.cloned.1.call-start = ((), (), s32[]{:S(2)}) async-start(), calls=%async_computation.5 | async-start | bytes 17825792 | tf_op jit(solution)/shard_map/all_gather | solution.py:76
  137.2 14.4 %all-to-all-start.1 = ((f32[16,16,512]{2,1,0:T(8,128)}), f32[16,16,512]{2,1,0:T(8,128)S(1)}, u32[]{:S(2)}, u32[]{:S(2)}) async-start(f32[16,16,512]{2,1,0:T(8,128)} %broadcast_in_dim.8), calls=%async_computation.1 | async-start | bytes 1048576 | tf_op jit(solution)/shard_map/all_to_all | solution.py:88
  179.1 21.6 %all-to-all-start.4 = ((f32[16,32,512]{2,1,0:T(8,128)}), f32[16,32,512]{2,1,0:T(8,128)S(1)}, u32[]{:S(2)}, u32[]{:S(2)}) async-start(f32[16,32,512]{2,1,0:T(8,128)} %broadcast_in_dim.10), calls=%async_computation.4 | async-start | bytes 2097152 | tf_op jit(solution)/shard_map/all_to_all | solution.py:88
Sparse Core Ops, SparseCore 0:
  9.8 98.2 all-gather.1

commit v4 on v3

--- a/solution.py
+++ b/solution.py
@@ -9,10 +9,9 @@
 GROUP = 8
 
 
-def factor_kernel(a_ref, r_ref, w_ref, head_ref):
+def factor_kernel(a_ref, r_ref, w_ref, head_ref, row_ref):
     n, width = a_ref.shape
     w_ref[...] = a_ref[...]
-    head_ref[...] = jnp.zeros(head_ref.shape, jnp.float32)
     subl = lax.broadcasted_iota(jnp.int32, (GROUP, 1), 0)
     for k in range(n // PANEL):
         base = k * PANEL
@@ -36,14 +35,19 @@
                 factor_col = jnp.where(subl > t, column * scale, 0.0)
                 block = block - factor_col * top
             r_ref[pl.ds(r0, GROUP), base:] = rows
-            head_ref[:, :GROUP] = jnp.transpose(rows[:, :PANEL])[:, :GROUP]
+            head = jnp.transpose(rows[:, :PANEL])
+            for t in range(GROUP):
+                row_ref[t, :, :span] = jnp.broadcast_to(rows[t:t + 1, :], (GROUP, span))
+                head_ref[t] = jnp.broadcast_to(head[:, t:t + 1], (PANEL, PANEL))
 
             def slab(s, c):
                 at = pl.multiple_of(base + s * GROUP, GROUP)
+                off = pl.multiple_of(s * GROUP, GROUP)
                 part = w_ref[pl.ds(at, GROUP), base:]
-                mult = head_ref[pl.ds(pl.multiple_of(s * GROUP, GROUP), GROUP), :]
                 for t in range(GROUP):
-                    part = part - mult[:, t:t + 1] * rows[t:t + 1, :]
+                    mult = head_ref[t, pl.ds(off, GROUP), :]
+                    mult = jnp.concatenate([mult] * (span // PANEL), axis=1)
+                    part = part - mult * row_ref[t, :, :span]
                 w_ref[pl.ds(at, GROUP), base:] = part
                 return c
 
@@ -66,7 +70,11 @@
         out_shape=jax.ShapeDtypeStruct((n, width), jnp.float32),
         in_specs=[pl.BlockSpec(memory_space=pltpu.VMEM)],
         out_specs=pl.BlockSpec(memory_space=pltpu.VMEM),
-        scratch_shapes=[pltpu.VMEM((n, width), jnp.float32), pltpu.VMEM((PANEL, PANEL), jnp.float32)],
+        scratch_shapes=[
+            pltpu.VMEM((n, width), jnp.float32),
+            pltpu.VMEM((GROUP, PANEL, PANEL), jnp.float32),
+            pltpu.VMEM((GROUP, GROUP, width), jnp.float32),
+        ],
     )(augmented)
 
 

time: 314 us -> 298 us (0.949)
  Pallas kernels: 97.9 us -> 81.9 us
    pallas_call x1, Pallas kernels: 97.9 us -> 81.9 us  [factor(): pl.pallas_call(factor_kernel, out_shape=jax.ShapeDtypeStruct((n, width),...]
where the time goes in v4:
time: 298 us; the launch traced here: 295 us
  waiting for transfers between devices  127 us (43%)
  Pallas kernels  81.9 us (27%)
  blocking collectives  40 us (13%)
  between operations  14.1 us (5%)
  matrix products  11.2 us (4%)
  starting transfers between devices  9.72 us (3%)
  local copies, waits for them, and re-layouts  8.08 us (3%)
    all_gather x1, waiting for transfers between devices, probe_product(): lax.all_gather(test_matrix, 'row', axis=0, tiled=True)  100 us
    pallas_call x1, Pallas kernels, factor(): pl.pallas_call(factor_kernel, out_shape=jax.ShapeDtypeStruct((n, width),...  81.9 us
    all_to_all x2, blocking collectives, scatter_sum(): return lax.all_to_all(pieces, axis, 0, 0, tiled=False).sum(0)  29.6 us
    all_to_all x2, waiting for transfers between devices, gather_rows(): gathered = lax.all_to_all(copies, axis, 0, 0, tiled=False)  26.1 us
    dot_general x1, matrix products, probe_product(): jnp.dot(matrix, lax.all_gather(test_matrix, 'row', axis=0, tiled=True), p...  10.5 us
    all_to_all x1, blocking collectives, gather_rows(): gathered = lax.all_to_all(copies, axis, 0, 0, tiled=False)  10.4 us
    all_to_all x2, starting transfers between devices, gather_rows(): gathered = lax.all_to_all(copies, axis, 0, 0, tiled=False)  9.68 us
  transfers between devices with their start and end apart: 3, of which 3 were waited for; matrix products, arithmetic and copies ran while one was open for 0% of the time, Pallas kernels for 0%

profile of v4, /device:TPU:2, one launch (start us, length us, event | category | flops | bytes accessed | tf_op | source)
XLA Modules:
  0.0 295.0 jit_solution(16270051940743432626)
XLA Ops:
  7.2 0.0 all-gather.2.cloned.1.call-start
  7.2 0.7 all-gather.2.cloned.1.call-update
  7.9 100.2 %all-gather.2.cloned.1.call-done = bf16[16384,512]{1,0:T(8,128)(2,1)} async-done(((bf16[1024,512]{1,0:T(8,128)(2,1)}), bf16[16384,512]{1,0:T(8,128)(2,1)}) %all-gather.2.cloned.1.call-update) | async-done | bytes 16777232 | tf_op jit(solution)/shard_map/all_gather | solution.py:84
  108.1 10.5 %fusion.4 = f32[256,512]{1,0:T(8,128)S(1)} fusion(bf16[256,16384]{1,0:T(8,128)(2,1)} %param.2, bf16[16384,512]{1,0:T(8,128)(2,1)} %all-gather.2.cloned.1.call-done), kind=kOutput, calls=%fused_computation.8 | convolution fusion | flops 4294967296 | bytes 25690112 | tf_op jit(solution)/shard_map/dot_general | solution.py:82
  118.6 17.7 %all_to_all.25 = f32[16,16,512]{2,1,0:T(8,128)S(1)} all-to-all(f32[16,16,512]{2,1,0:T(8,128)S(1)} %bitcast.30), channel_id=1, replica_groups=mesh['row'=16,'col'=16] {'col'}, dimensions={0} | all-to-all | bytes 1048576 | tf_op jit(solution)/shard_map/all_to_all | solution.py:91
  136.3 0.9 broadcast_in_dim.8
  137.2 4.8 %all-to-all-start.1 = ((f32[16,16,512]{2,1,0:T(8,128)}), f32[16,16,512]{2,1,0:T(8,128)S(1)}, u32[]{:S(2)}, u32[]{:S(2)}) async-start(f32[16,16,512]{2,1,0:T(8,128)} %broadcast_in_dim.8), calls=%async_computation.1 | async-start | bytes 1048576 | tf_op jit(solution)/shard_map/all_to_all | solution.py:96
  142.0 9.6 %all-to-all-done.1 = f32[16,16,512]{2,1,0:T(8,128)S(1)} async-done(((f32[16,16,512]{2,1,0:T(8,128)}), f32[16,16,512]{2,1,0:T(8,128)S(1)}, u32[]{:S(2)}, u32[]{:S(2)}) %all-to-all-start.1) | async-done | bytes 524320 | tf_op jit(solution)/shard_map/all_to_all | solution.py:96
  151.6 0.2 copy.16
  151.8 0.7 fusion
  152.5 0.2 reshape.25
  152.6 12.0 %all_to_all.26 = f32[16,1,1024]{2,1,0:T(1,128)S(1)} all-to-all(f32[16,1,1024]{2,1,0:T(1,128)S(1)} %reshape.25), channel_id=1, replica_groups=mesh['row'=16,'col'=16] {'row'}, dimensions={0} | all-to-all | bytes 131072 | tf_op jit(solution)/shard_map/all_to_all | solution.py:91
  164.6 0.5 broadcast.10
  165.1 0.8 reduce
  165.9 0.1 reshape.26
  166.1 0.1 copy.18
  166.2 0.2 reshape.27
  166.4 10.4 %all_to_all.27 = f32[16,1,1024]{2,1,0:T(1,128)S(1)} all-to-all(f32[16,1,1024]{2,1,0:T(1,128)S(1)} %reshape.27), channel_id=1, replica_groups=mesh['row'=16,'col'=16] {'row'}, dimensions={0} | all-to-all | bytes 131072 | tf_op jit(solution)/shard_map/all_to_all | solution.py:96
  176.7 0.8 reduce.1
  177.6 0.1 reshape.28
  177.7 0.2 copy.19
  177.8 0.1 reshape.23
  178.0 1.1 broadcast_in_dim.10
  179.1 4.9 %all-to-all-start.4 = ((f32[16,32,512]{2,1,0:T(8,128)}), f32[16,32,512]{2,1,0:T(8,128)S(1)}, u32[]{:S(2)}, u32[]{:S(2)}) async-start(f32[16,32,512]{2,1,0:T(8,128)} %broadcast_in_dim.10), calls=%async_computation.4 | async-start | bytes 2097152 | tf_op jit(solution)/shard_map/all_to_all | solution.py:96
  183.9 0.1 pad.2.clone
  184.0 0.1 copy.21
  184.1 16.5 %all-to-all-done.4 = f32[16,32,512]{2,1,0:T(8,128)S(1)} async-done(((f32[16,32,512]{2,1,0:T(8,128)}), f32[16,32,512]{2,1,0:T(8,128)S(1)}, u32[]{:S(2)}, u32[]{:S(2)}) %all-to-all-start.4) | async-done | bytes 1048608 | tf_op jit(solution)/shard_map/all_to_all | solution.py:96
  200.6 0.1 broadcast_multiply_fusion
  200.7 0.3 copy.20
  201.1 1.2 maximum_maximum_fusion.a_ref
  202.3 81.9 %shard_map.41 = f32[512,640]{1,0:T(8,128)} custom-call(f32[512,640]{1,0:T(8,128)} %maximum_maximum_fusion.a_ref), custom_call_target="tpu_custom_call" | custom-call | tf_op jit(solution)/shard_map/pallas_call | solution.py:68
  284.2 1.0 slice_bitcast_fusion
  285.2 2.3 slice.9
  287.5 0.7 copy.22
  (4 shorter events, 0.1 us)
Async XLA Ops:
  7.2 101.0 %all-gather.2.cloned.1.call-start = ((), (), s32[]{:S(2)}) async-start(), calls=%async_computation.5 | async-start | bytes 17825792 | tf_op jit(solution)/shard_map/all_gather | solution.py:84
  137.2 14.4 %all-to-all-start.1 = ((f32[16,16,512]{2,1,0:T(8,128)}), f32[16,16,512]{2,1,0:T(8,128)S(1)}, u32[]{:S(2)}, u32[]{:S(2)}) async-start(f32[16,16,512]{2,1,0:T(8,128)} %broadcast_in_dim.8), calls=%async_computation.1 | async-start | bytes 1048576 | tf_op jit(solution)/shard_map/all_to_all | solution.py:96
  179.1 21.6 %all-to-all-start.4 = ((f32[16,32,512]{2,1,0:T(8,128)}), f32[16,32,512]{2,1,0:T(8,128)S(1)}, u32[]{:S(2)}, u32[]{:S(2)}) async-start(f32[16,32,512]{2,1,0:T(8,128)} %broadcast_in_dim.10), calls=%async_computation.4 | async-start | bytes 2097152 | tf_op jit(solution)/shard_map/all_to_all | solution.py:96
Sparse Core Ops, SparseCore 0:
  9.8 98.2 all-gather.1

commit v5 on v4

--- a/solution.py
+++ b/solution.py
@@ -6,6 +6,7 @@
 from jax.sharding import PartitionSpec as P
 
 PANEL = 128
+CHUNKS = 2
 GROUP = 8
 
 
@@ -102,9 +103,15 @@
     n_row = lax.axis_size("row")
     total_rows = matrix.shape[0] * n_row
     k = test_matrix.shape[1]
-    partial_value = probe_product(matrix, test_matrix)
-    own_rows = scatter_sum(partial_value, "col", n_col)
-    sketch = gather_rows(own_rows, "col", n_col)
+    step = k // CHUNKS
+    own_parts, sketch_parts = [], []
+    for h in range(CHUNKS):
+        partial_value = probe_product(matrix, test_matrix[:, h * step:(h + 1) * step])
+        own_part = scatter_sum(partial_value, "col", n_col)
+        own_parts.append(own_part)
+        sketch_parts.append(gather_rows(own_part, "col", n_col))
+    own_rows = jnp.concatenate(own_parts, axis=1)
+    sketch = jnp.concatenate(sketch_parts, axis=1)
     width = k // n_col
     col = lax.axis_index("col")
     columns = lax.dynamic_slice_in_dim(sketch, col * width, width, 1)

time: 298 us -> 322 us (1.081)
  starting transfers between devices: 9.72 us -> 29.1 us
  blocking collectives: 40 us -> 22.4 us
  waiting for transfers between devices: 127 us -> 139 us
  matrix products: 11.2 us -> 18.1 us
    all_to_all x2 -> x1, blocking collectives: 29.6 us -> 12 us  [scatter_sum(): return lax.all_to_all(pieces, axis, 0, 0, tiled=False).sum(0)]
    all_to_all x0 -> x2, starting transfers between devices: none -> 14.5 us  [scatter_sum(): return lax.all_to_all(pieces, axis, 0, 0, tiled=False).sum(0)]
    all_to_all x0 -> x2, waiting for transfers between devices: none -> 7.7 us  [scatter_sum(): return lax.all_to_all(pieces, axis, 0, 0, tiled=False).sum(0)]
    dot_general x1 -> x2, matrix products: 10.5 us -> 17.6 us  [probe_product(): jnp.dot(matrix, lax.all_gather(test_matrix, 'row', axis=0, tiled=True), p...]
    all_to_all x2 -> x3, waiting for transfers between devices: 26.1 us -> 31.3 us  [gather_rows(): gathered = lax.all_to_all(copies, axis, 0, 0, tiled=False)]
    all_to_all x2 -> x3, starting transfers between devices: 9.68 us -> 14.5 us  [gather_rows(): gathered = lax.all_to_all(copies, axis, 0, 0, tiled=False)]
    all_gather x1 -> x2, waiting for transfers between devices: 100 us -> 99.2 us  [probe_product(): lax.all_gather(test_matrix, 'row', axis=0, tiled=True)]
  transfers between devices with their start and end apart: 3 -> 7, of which waited for: 3 -> 6; matrix products, arithmetic and copies ran while one was open for 0% -> 6% of each run, Pallas kernels for 0% -> 0%
where the time goes in v5:
time: 322 us; the launch traced here: 318 us
  waiting for transfers between devices  139 us (43%)
  Pallas kernels  81.9 us (25%)
  starting transfers between devices  29.1 us (9%)
  blocking collectives  22.4 us (7%)
  matrix products  18.1 us (6%)
  between operations  14.2 us (4%)
  local copies, waits for them, and re-layouts  10.9 us (3%)
    all_gather x2, waiting for transfers between devices, probe_product(): lax.all_gather(test_matrix, 'row', axis=0, tiled=True)  99.2 us
    pallas_call x1, Pallas kernels, factor(): pl.pallas_call(factor_kernel, out_shape=jax.ShapeDtypeStruct((n, width),...  81.9 us
    all_to_all x3, waiting for transfers between devices, gather_rows(): gathered = lax.all_to_all(copies, axis, 0, 0, tiled=False)  31.3 us
    dot_general x2, matrix products, probe_product(): jnp.dot(matrix, lax.all_gather(test_matrix, 'row', axis=0, tiled=True), p...  17.6 us
    all_to_all x2, starting transfers between devices, scatter_sum(): return lax.all_to_all(pieces, axis, 0, 0, tiled=False).sum(0)  14.5 us
    all_to_all x3, starting transfers between devices, gather_rows(): gathered = lax.all_to_all(copies, axis, 0, 0, tiled=False)  14.5 us
    all_to_all x1, blocking collectives, scatter_sum(): return lax.all_to_all(pieces, axis, 0, 0, tiled=False).sum(0)  12 us
    all_to_all x1, blocking collectives, gather_rows(): gathered = lax.all_to_all(copies, axis, 0, 0, tiled=False)  10.4 us
  transfers between devices with their start and end apart: 7, of which 6 were waited for; matrix products, arithmetic and copies ran while one was open for 6% of the time, Pallas kernels for 0%

profile of v5, /device:TPU:2, one launch (start us, length us, event | category | flops | bytes accessed | tf_op | source)
XLA Modules:
  0.0 318.3 jit_solution(7224073887777900908)
XLA Ops:
  7.2 0.0 all-gather.5.cloned.1.call-start
  7.2 2.2 fusion.5
  9.4 0.0 all-gather.5.cloned.1.call-update
  9.5 0.0 all-gather.3.cloned.1.call-start
  9.5 0.7 all-gather.3.cloned.1.call-update
  10.2 58.4 %all-gather.5.cloned.1.call-done = bf16[16384,256]{1,0:T(8,128)(2,1)} async-done(((bf16[1024,256]{1,0:T(8,128)(2,1)}), bf16[16384,256]{1,0:T(8,128)(2,1)}) %all-gather.5.cloned.1.call-update) | async-done | bytes 8388624 | tf_op jit(solution)/shard_map/all_gather | solution.py:85
  68.6 8.8 %fusion.7 = f32[256,256]{1,0:T(8,128)} fusion(bf16[256,16384]{1,0:T(8,128)(2,1)} %param.2, bf16[16384,256]{1,0:T(8,128)(2,1)} %all-gather.5.cloned.1.call-done), kind=kOutput, calls=%fused_computation.16 | convolution fusion | flops 2147483648 | bytes 17039360 | tf_op jit(solution)/shard_map/dot_general | solution.py:83
  77.4 7.3 %all-to-all-start.2 = ((f32[16,16,256]{2,1,0:T(8,128)}), f32[16,16,256]{2,1,0:T(8,128)S(1)}, u32[]{:S(2)}, u32[]{:S(2)}) async-start(f32[16,16,256]{2,1,0:T(8,128)} %bitcast.2), calls=%async_computation.2 | async-start | bytes 524288 | tf_op jit(solution)/shard_map/all_to_all | solution.py:92
  84.7 40.8 %all-gather.3.cloned.1.call-done = bf16[16384,256]{1,0:T(8,128)(2,1)} async-done(((bf16[1024,256]{1,0:T(8,128)(2,1)}), bf16[16384,256]{1,0:T(8,128)(2,1)}) %all-gather.3.cloned.1.call-update) | async-done | bytes 8388624 | tf_op jit(solution)/shard_map/all_gather | solution.py:85
  125.5 8.8 %fusion.6 = f32[256,256]{1,0:T(8,128)} fusion(bf16[256,16384]{1,0:T(8,128)(2,1)} %param.2, bf16[16384,256]{1,0:T(8,128)(2,1)} %all-gather.3.cloned.1.call-done), kind=kOutput, calls=%fused_computation.15 | convolution fusion | flops 2147483648 | bytes 17039360 | tf_op jit(solution)/shard_map/dot_general | solution.py:83
  134.3 0.0 all-to-all-done.2
  134.3 7.3 %all-to-all-start = ((f32[16,16,256]{2,1,0:T(8,128)}), f32[16,16,256]{2,1,0:T(8,128)S(1)}, u32[]{:S(2)}, u32[]{:S(2)}) async-start(f32[16,16,256]{2,1,0:T(8,128)} %bitcast), calls=%async_computation | async-start | bytes 524288 | tf_op jit(solution)/shard_map/all_to_all | solution.py:92
  141.6 7.7 %all-to-all-done = f32[16,16,256]{2,1,0:T(8,128)S(1)} async-done(((f32[16,16,256]{2,1,0:T(8,128)}), f32[16,16,256]{2,1,0:T(8,128)S(1)}, u32[]{:S(2)}, u32[]{:S(2)}) %all-to-all-start) | async-done | bytes 262176 | tf_op jit(solution)/shard_map/all_to_all | solution.py:92
  149.3 0.7 broadcast_in_dim.11
  150.0 4.8 %all-to-all-start.3 = ((f32[16,16,256]{2,1,0:T(8,128)}), f32[16,16,256]{2,1,0:T(8,128)S(1)}, u32[]{:S(2)}, u32[]{:S(2)}) async-start(f32[16,16,256]{2,1,0:T(8,128)} %broadcast_in_dim.11), calls=%async_computation.3 | async-start | bytes 524288 | tf_op jit(solution)/shard_map/all_to_all | solution.py:97
  154.8 7.4 %all-to-all-done.3 = f32[16,16,256]{2,1,0:T(8,128)S(1)} async-done(((f32[16,16,256]{2,1,0:T(8,128)}), f32[16,16,256]{2,1,0:T(8,128)S(1)}, u32[]{:S(2)}, u32[]{:S(2)}) %all-to-all-start.3) | async-done | bytes 262176 | tf_op jit(solution)/shard_map/all_to_all | solution.py:97
  162.2 0.7 broadcast_in_dim.10
  162.9 4.8 %all-to-all-start.1 = ((f32[16,16,256]{2,1,0:T(8,128)}), f32[16,16,256]{2,1,0:T(8,128)S(1)}, u32[]{:S(2)}, u32[]{:S(2)}) async-start(f32[16,16,256]{2,1,0:T(8,128)} %broadcast_in_dim.10), calls=%async_computation.1 | async-start | bytes 524288 | tf_op jit(solution)/shard_map/all_to_all | solution.py:97
  167.7 7.4 %all-to-all-done.1 = f32[16,16,256]{2,1,0:T(8,128)S(1)} async-done(((f32[16,16,256]{2,1,0:T(8,128)}), f32[16,16,256]{2,1,0:T(8,128)S(1)}, u32[]{:S(2)}, u32[]{:S(2)}) %all-to-all-start.1) | async-done | bytes 262176 | tf_op jit(solution)/shard_map/all_to_all | solution.py:97
  175.1 0.5 fusion
  175.6 0.1 reshape.33
  175.7 0.1 copy.21
  175.8 0.2 reshape.35
  176.0 12.0 %all_to_all.35 = f32[16,1,1024]{2,1,0:T(1,128)S(1)} all-to-all(f32[16,1,1024]{2,1,0:T(1,128)S(1)} %reshape.35), channel_id=1, replica_groups=mesh['row'=16,'col'=16] {'row'}, dimensions={0} | all-to-all | bytes 131072 | tf_op jit(solution)/shard_map/all_to_all | solution.py:92
  188.0 0.5 broadcast.11
  188.5 0.8 reduce
  189.3 0.1 reshape.36
  189.4 0.2 reshape.37
  189.6 10.4 %all_to_all.36 = f32[16,1,1024]{2,1,0:T(1,128)S(1)} all-to-all(f32[16,1,1024]{2,1,0:T(1,128)S(1)} %reshape.37), channel_id=1, replica_groups=mesh['row'=16,'col'=16] {'row'}, dimensions={0} | all-to-all | bytes 131072 | tf_op jit(solution)/shard_map/all_to_all | solution.py:97
  200.0 0.8 reduce.1
  200.8 0.1 reshape.38
  200.9 0.2 copy.16
  201.1 0.1 reshape.34
  201.2 1.1 broadcast_in_dim.13
  202.3 4.9 %all-to-all-start.6 = ((f32[16,32,512]{2,1,0:T(8,128)}), f32[16,32,512]{2,1,0:T(8,128)S(1)}, u32[]{:S(2)}, u32[]{:S(2)}) async-start(f32[16,32,512]{2,1,0:T(8,128)} %broadcast_in_dim.13), calls=%async_computation.6 | async-start | bytes 2097152 | tf_op jit(solution)/shard_map/all_to_all | solution.py:97
  207.2 0.1 pad.2.clone
  207.3 0.1 copy.18
  207.4 16.5 %all-to-all-done.6 = f32[16,32,512]{2,1,0:T(8,128)S(1)} async-done(((f32[16,32,512]{2,1,0:T(8,128)}), f32[16,32,512]{2,1,0:T(8,128)S(1)}, u32[]{:S(2)}, u32[]{:S(2)}) %all-to-all-start.6) | async-done | bytes 1048608 | tf_op jit(solution)/shard_map/all_to_all | solution.py:97
  223.9 0.1 broadcast_multiply_fusion
  224.0 0.3 copy.17
  224.4 1.2 maximum_maximum_fusion.a_ref
  225.6 81.9 %shard_map.41 = f32[512,640]{1,0:T(8,128)} custom-call(f32[512,640]{1,0:T(8,128)} %maximum_maximum_fusion.a_ref), custom_call_target="tpu_custom_call" | custom-call | tf_op jit(solution)/shard_map/pallas_call | solution.py:69
  307.5 1.0 slice_bitcast_fusion
  308.5 2.3 slice.17
  310.8 0.7 copy.19
  (6 shorter events, 0.1 us)
Async XLA Ops:
  7.2 61.5 %all-gather.5.cloned.1.call-start = ((), (), s32[]{:S(2)}) async-start(), calls=%async_computation.8 | async-start | bytes 8912896 | tf_op jit(solution)/shard_map/all_gather | solution.py:85
  9.5 116.0 %all-gather.3.cloned.1.call-start = ((), (), s32[]{:S(2)}) async-start(), calls=%async_computation.7 | async-start | bytes 8912896 | tf_op jit(solution)/shard_map/all_gather | solution.py:85
  77.4 56.8 %all-to-all-start.2 = ((f32[16,16,256]{2,1,0:T(8,128)}), f32[16,16,256]{2,1,0:T(8,128)S(1)}, u32[]{:S(2)}, u32[]{:S(2)}) async-start(f32[16,16,256]{2,1,0:T(8,128)} %bitcast.2), calls=%async_computation.2 | async-start | bytes 524288 | tf_op jit(solution)/shard_map/all_to_all | solution.py:92
  134.3 15.0 %all-to-all-start = ((f32[16,16,256]{2,1,0:T(8,128)}), f32[16,16,256]{2,1,0:T(8,128)S(1)}, u32[]{:S(2)}, u32[]{:S(2)}) async-start(f32[16,16,256]{2,1,0:T(8,128)} %bitcast), calls=%async_computation | async-start | bytes 524288 | tf_op jit(solution)/shard_map/all_to_all | solution.py:92
  150.0 12.2 %all-to-all-start.3 = ((f32[16,16,256]{2,1,0:T(8,128)}), f32[16,16,256]{2,1,0:T(8,128)S(1)}, u32[]{:S(2)}, u32[]{:S(2)}) async-start(f32[16,16,256]{2,1,0:T(8,128)} %broadcast_in_dim.11), calls=%async_computation.3 | async-start | bytes 524288 | tf_op jit(solution)/shard_map/all_to_all | solution.py:97
  162.9 12.2 %all-to-all-start.1 = ((f32[16,16,256]{2,1,0:T(8,128)}), f32[16,16,256]{2,1,0:T(8,128)S(1)}, u32[]{:S(2)}, u32[]{:S(2)}) async-start(f32[16,16,256]{2,1,0:T(8,128)} %broadcast_in_dim.10), calls=%async_computation.1 | async-start | bytes 524288 | tf_op jit(solution)/shard_map/all_to_all | solution.py:97
  202.3 21.6 %all-to-all-start.6 = ((f32[16,32,512]{2,1,0:T(8,128)}), f32[16,32,512]{2,1,0:T(8,128)S(1)}, u32[]{:S(2)}, u32[]{:S(2)}) async-start(f32[16,32,512]{2,1,0:T(8,128)} %broadcast_in_dim.13), calls=%async_computation.6 | async-start | bytes 2097152 | tf_op jit(solution)/shard_map/all_to_all | solution.py:97
Sparse Core Ops, SparseCore 0:
  9.8 58.7 all-gather.4
  71.0 54.3 all-gather.2

commit v6 on v4

--- a/solution.py
+++ b/solution.py
@@ -6,13 +6,16 @@
 from jax.sharding import PartitionSpec as P
 
 PANEL = 128
-GROUP = 8
+GROUP = 32
 
 
-def factor_kernel(a_ref, r_ref, w_ref, head_ref, row_ref):
-    n, width = a_ref.shape
-    w_ref[...] = a_ref[...]
+def factor_kernel(a_ref, e_ref, r_ref, x_ref, w_ref, head_ref, row_ref):
+    n = a_ref.shape[0]
+    width = n + e_ref.shape[1]
+    w_ref[:, :n] = a_ref[...]
+    w_ref[:, n:] = e_ref[...]
     subl = lax.broadcasted_iota(jnp.int32, (GROUP, 1), 0)
+    tile = lax.broadcasted_iota(jnp.int32, (1, PANEL), 1)
     for k in range(n // PANEL):
         base = k * PANEL
         span = width - base
@@ -23,18 +26,22 @@
         def group(g, carry, base=base, span=span, lanes=lanes):
             r0 = pl.multiple_of(base + g * GROUP, GROUP)
             block = w_ref[pl.ds(r0, GROUP), base:]
+            diag = pltpu.roll(block[:, :PANEL], (PANEL - g * GROUP) % PANEL, 1)
             rows = jnp.zeros((GROUP, span), jnp.float32)
             for t in range(GROUP):
                 j = r0 + t
-                column = jnp.sum(jnp.where(lanes[:, :PANEL] == j, block[:, :PANEL], 0.0), axis=1, keepdims=True)
+                column = diag[:, t:t + 1]
                 pivot = column[t:t + 1, :]
                 scale = lax.rsqrt(pivot)
                 scale = scale * (1.5 - 0.5 * pivot * scale * scale)
+                factor_col = jnp.where(subl > t, column * scale, 0.0)
+                near = jnp.where(tile >= t, diag[t:t + 1, :] * scale, 0.0)
+                diag = diag - factor_col * near
                 top = jnp.where(lanes[:1] >= j, block[t:t + 1, :] * scale, 0.0)
                 rows = jnp.where(subl == t, top, rows)
-                factor_col = jnp.where(subl > t, column * scale, 0.0)
                 block = block - factor_col * top
-            r_ref[pl.ds(r0, GROUP), base:] = rows
+            r_ref[pl.ds(r0, GROUP), base:] = rows[:, :n - base]
+            x_ref[pl.ds(r0, GROUP), :] = rows[:, n - base:]
             head = jnp.transpose(rows[:, :PANEL])
             for t in range(GROUP):
                 row_ref[t, :, :span] = jnp.broadcast_to(rows[t:t + 1, :], (GROUP, span))
@@ -57,25 +64,27 @@
         lax.fori_loop(0, PANEL // GROUP, group, 0)
         rest = base + PANEL
         if rest < n:
-            block = r_ref[base:rest, rest:]
-            left = jnp.transpose(block[:, :n - rest])
+            left = r_ref[base:rest, rest:]
+            block = jnp.concatenate([left, x_ref[base:rest, :]], axis=1)
+            left = jnp.transpose(left)
             update = jnp.dot(left, block, precision=lax.Precision.HIGHEST, preferred_element_type=jnp.float32)
             w_ref[rest:n, rest:] = w_ref[rest:n, rest:] - update
 
 
-def factor(augmented):
-    n, width = augmented.shape
+def factor(gram, extra):
+    n, more = gram.shape[0], extra.shape[1]
+    width = n + more
     return pl.pallas_call(
         factor_kernel,
-        out_shape=jax.ShapeDtypeStruct((n, width), jnp.float32),
-        in_specs=[pl.BlockSpec(memory_space=pltpu.VMEM)],
-        out_specs=pl.BlockSpec(memory_space=pltpu.VMEM),
+        out_shape=(jax.ShapeDtypeStruct((n, n), jnp.float32), jax.ShapeDtypeStruct((n, more), jnp.float32)),
+        in_specs=[pl.BlockSpec(memory_space=pltpu.VMEM)] * 2,
+        out_specs=(pl.BlockSpec(memory_space=pltpu.VMEM),) * 2,
         scratch_shapes=[
             pltpu.VMEM((n, width), jnp.float32),
             pltpu.VMEM((GROUP, PANEL, PANEL), jnp.float32),
             pltpu.VMEM((GROUP, GROUP, width), jnp.float32),
         ],
-    )(augmented)
+    )(gram, extra)
 
 
 def probe_product(matrix, test_matrix):
@@ -110,12 +119,11 @@
     columns = lax.dynamic_slice_in_dim(sketch, col * width, width, 1)
     gram_part = jnp.dot(sketch.T, columns, precision=lax.Precision.HIGHEST)
     gram_part = gather_rows(scatter_sum(gram_part, "row", n_row), "row", n_row)
-    blocks = gather_rows(gram_part.T, "col", n_col)
-    gram = blocks.T / jnp.float32(total_rows)
+    gram = gather_rows(gram_part.T, "col", n_col) / jnp.float32(total_rows)
     share = own_rows.shape[0]
-    pad = jnp.zeros((k, PANEL - share), jnp.float32)
-    factored = factor(jnp.concatenate([gram, own_rows.T, pad], axis=1))
-    return (factored[:, k:k + share].T, factored[:, :k])
+    extra = jnp.concatenate([own_rows.T, jnp.zeros((k, PANEL - share), jnp.float32)], axis=1)
+    upper, solved = factor(gram, extra)
+    return (solved[:, :share].T, upper)
 
 
 def solution(mesh):

time: 298 us -> 282 us (0.946)
  Pallas kernels: 81.9 us -> 68.6 us
    pallas_call x1, Pallas kernels: 81.9 us -> 68.6 us  [factor(): pl.pallas_call(factor_kernel, out_shape=(jax.ShapeDtypeStruct((n, n), jnp...]
where the time goes in v6:
time: 282 us; the launch traced here: 279 us
  waiting for transfers between devices  126 us (45%)
  Pallas kernels  68.6 us (24%)
  blocking collectives  40 us (14%)
  between operations  14.1 us (5%)
  matrix products  11.2 us (4%)
  starting transfers between devices  9.72 us (3%)
  local copies, waits for them, and re-layouts  6.15 us (2%)
    all_gather x1, waiting for transfers between devices, probe_product(): lax.all_gather(test_matrix, 'row', axis=0, tiled=True)  100 us
    pallas_call x1, Pallas kernels, factor(): pl.pallas_call(factor_kernel, out_shape=(jax.ShapeDtypeStruct((n, n), jnp...  68.6 us
    all_to_all x2, blocking collectives, scatter_sum(): return lax.all_to_all(pieces, axis, 0, 0, tiled=False).sum(0)  29.6 us
    all_to_all x2, waiting for transfers between devices, gather_rows(): gathered = lax.all_to_all(copies, axis, 0, 0, tiled=False)  25.4 us
    dot_general x1, matrix products, probe_product(): jnp.dot(matrix, lax.all_gather(test_matrix, 'row', axis=0, tiled=True), p...  10.5 us
    all_to_all x1, blocking collectives, gather_rows(): gathered = lax.all_to_all(copies, axis, 0, 0, tiled=False)  10.4 us
    all_to_all x2, starting transfers between devices, gather_rows(): gathered = lax.all_to_all(copies, axis, 0, 0, tiled=False)  9.68 us
  transfers between devices with their start and end apart: 3, of which 3 were waited for; matrix products, arithmetic and copies ran while one was open for 0% of the time, Pallas kernels for 0%

profile of v6, /device:TPU:2, one launch (start us, length us, event | category | flops | bytes accessed | tf_op | source)
XLA Modules:
  0.0 278.9 jit_solution(10382343579401021641)
XLA Ops:
  7.2 0.0 all-gather.2.cloned.1.call-start
  7.2 0.7 all-gather.2.cloned.1.call-update
  7.9 100.2 %all-gather.2.cloned.1.call-done = bf16[16384,512]{1,0:T(8,128)(2,1)} async-done(((bf16[1024,512]{1,0:T(8,128)(2,1)}), bf16[16384,512]{1,0:T(8,128)(2,1)}) %all-gather.2.cloned.1.call-update) | async-done | bytes 16777232 | tf_op jit(solution)/shard_map/all_gather | solution.py:93
  108.1 10.5 %fusion.4 = f32[256,512]{1,0:T(8,128)S(1)} fusion(bf16[256,16384]{1,0:T(8,128)(2,1)} %param.2, bf16[16384,512]{1,0:T(8,128)(2,1)} %all-gather.2.cloned.1.call-done), kind=kOutput, calls=%fused_computation.7 | convolution fusion | flops 4294967296 | bytes 25690112 | tf_op jit(solution)/shard_map/dot_general | solution.py:91
  118.6 17.7 %all_to_all.25 = f32[16,16,512]{2,1,0:T(8,128)S(1)} all-to-all(f32[16,16,512]{2,1,0:T(8,128)S(1)} %bitcast.28), channel_id=1, replica_groups=mesh['row'=16,'col'=16] {'col'}, dimensions={0} | all-to-all | bytes 1048576 | tf_op jit(solution)/shard_map/all_to_all | solution.py:100
  136.3 0.9 broadcast_in_dim.6
  137.2 4.8 %all-to-all-start.1 = ((f32[16,16,512]{2,1,0:T(8,128)}), f32[16,16,512]{2,1,0:T(8,128)S(1)}, u32[]{:S(2)}, u32[]{:S(2)}) async-start(f32[16,16,512]{2,1,0:T(8,128)} %broadcast_in_dim.6), calls=%async_computation.1 | async-start | bytes 1048576 | tf_op jit(solution)/shard_map/all_to_all | solution.py:105
  142.0 9.6 %all-to-all-done.1 = f32[16,16,512]{2,1,0:T(8,128)S(1)} async-done(((f32[16,16,512]{2,1,0:T(8,128)}), f32[16,16,512]{2,1,0:T(8,128)S(1)}, u32[]{:S(2)}, u32[]{:S(2)}) %all-to-all-start.1) | async-done | bytes 524320 | tf_op jit(solution)/shard_map/all_to_all | solution.py:105
  151.6 0.2 copy.14
  151.8 0.7 fusion
  152.5 0.2 reshape.25
  152.7 12.0 %all_to_all.26 = f32[16,1,1024]{2,1,0:T(1,128)S(1)} all-to-all(f32[16,1,1024]{2,1,0:T(1,128)S(1)} %reshape.25), channel_id=1, replica_groups=mesh['row'=16,'col'=16] {'row'}, dimensions={0} | all-to-all | bytes 131072 | tf_op jit(solution)/shard_map/all_to_all | solution.py:100
  164.6 0.5 broadcast.8
  165.1 0.8 reduce
  165.9 0.1 reshape.26
  166.1 0.1 copy.16
  166.2 0.2 reshape.27
  166.4 10.4 %all_to_all.27 = f32[16,1,1024]{2,1,0:T(1,128)S(1)} all-to-all(f32[16,1,1024]{2,1,0:T(1,128)S(1)} %reshape.27), channel_id=1, replica_groups=mesh['row'=16,'col'=16] {'row'}, dimensions={0} | all-to-all | bytes 131072 | tf_op jit(solution)/shard_map/all_to_all | solution.py:105
  176.7 0.8 reduce.1
  177.5 0.1 reshape.28
  177.7 0.2 copy.17
  177.8 0.1 reshape.23
  178.0 1.1 broadcast_in_dim.8
  179.1 4.9 %all-to-all-start.4 = ((f32[16,32,512]{2,1,0:T(8,128)}), f32[16,32,512]{2,1,0:T(8,128)S(1)}, u32[]{:S(2)}, u32[]{:S(2)}) async-start(f32[16,32,512]{2,1,0:T(8,128)} %broadcast_in_dim.8), calls=%async_computation.4 | async-start | bytes 2097152 | tf_op jit(solution)/shard_map/all_to_all | solution.py:105
  183.9 0.1 copy.18
  184.0 0.7 concatenate.3.e_ref
  184.8 15.8 %all-to-all-done.4 = f32[16,32,512]{2,1,0:T(8,128)S(1)} async-done(((f32[16,32,512]{2,1,0:T(8,128)}), f32[16,32,512]{2,1,0:T(8,128)S(1)}, u32[]{:S(2)}, u32[]{:S(2)}) %all-to-all-start.4) | async-done | bytes 1048608 | tf_op jit(solution)/shard_map/all_to_all | solution.py:105
  200.6 1.1 broadcast_multiply_fusion
  201.8 68.6 %shard_map.41 = (f32[512,512]{1,0:T(8,128)}, f32[512,128]{1,0:T(8,128)}) custom-call(f32[512,512]{1,0:T(8,128)} %bitcast.22, f32[512,128]{1,0:T(8,128)} %concatenate.3.e_ref), custom_call_target="tpu_custom_call" | custom-call | tf_op jit(solution)/shard_map/pallas_call | solution.py:77
  270.4 1.0 slice_bitcast_fusion
  271.4 0.7 copy.19
  (3 shorter events, 0.1 us)
Async XLA Ops:
  7.2 101.0 %all-gather.2.cloned.1.call-start = ((), (), s32[]{:S(2)}) async-start(), calls=%async_computation.5 | async-start | bytes 17825792 | tf_op jit(solution)/shard_map/all_gather | solution.py:93
  137.2 14.4 %all-to-all-start.1 = ((f32[16,16,512]{2,1,0:T(8,128)}), f32[16,16,512]{2,1,0:T(8,128)S(1)}, u32[]{:S(2)}, u32[]{:S(2)}) async-start(f32[16,16,512]{2,1,0:T(8,128)} %broadcast_in_dim.6), calls=%async_computation.1 | async-start | bytes 1048576 | tf_op jit(solution)/shard_map/all_to_all | solution.py:105
  179.1 21.6 %all-to-all-start.4 = ((f32[16,32,512]{2,1,0:T(8,128)}), f32[16,32,512]{2,1,0:T(8,128)S(1)}, u32[]{:S(2)}, u32[]{:S(2)}) async-start(f32[16,32,512]{2,1,0:T(8,128)} %broadcast_in_dim.8), calls=%async_computation.4 | async-start | bytes 2097152 | tf_op jit(solution)/shard_map/all_to_all | solution.py:105
Sparse Core Ops, SparseCore 0:
  9.8 98.2 all-gather.1

commit v7 on v6

--- a/solution.py
+++ b/solution.py
@@ -15,53 +15,40 @@
     w_ref[:, :n] = a_ref[...]
     w_ref[:, n:] = e_ref[...]
     subl = lax.broadcasted_iota(jnp.int32, (GROUP, 1), 0)
-    tile = lax.broadcasted_iota(jnp.int32, (1, PANEL), 1)
     for k in range(n // PANEL):
         base = k * PANEL
         span = width - base
-        lanes = lax.broadcasted_iota(jnp.int32, (GROUP, span), 1) + base
+        lanes = lax.broadcasted_iota(jnp.int32, (1, span), 1) + base
         if base:
             r_ref[base:base + PANEL, :base] = jnp.zeros((PANEL, base), jnp.float32)
-
-        def group(g, carry, base=base, span=span, lanes=lanes):
-            r0 = pl.multiple_of(base + g * GROUP, GROUP)
-            block = w_ref[pl.ds(r0, GROUP), base:]
-            diag = pltpu.roll(block[:, :PANEL], (PANEL - g * GROUP) % PANEL, 1)
+        for g in range(PANEL // GROUP):
+            r0 = base + g * GROUP
+            block = w_ref[r0:r0 + GROUP, base:]
             rows = jnp.zeros((GROUP, span), jnp.float32)
             for t in range(GROUP):
                 j = r0 + t
-                column = diag[:, t:t + 1]
+                column = block[:, j - base:j - base + 1]
                 pivot = column[t:t + 1, :]
                 scale = lax.rsqrt(pivot)
-                scale = scale * (1.5 - 0.5 * pivot * scale * scale)
                 factor_col = jnp.where(subl > t, column * scale, 0.0)
-                near = jnp.where(tile >= t, diag[t:t + 1, :] * scale, 0.0)
-                diag = diag - factor_col * near
-                top = jnp.where(lanes[:1] >= j, block[t:t + 1, :] * scale, 0.0)
+                top = jnp.where(lanes >= j, block[t:t + 1, :] * scale, 0.0)
                 rows = jnp.where(subl == t, top, rows)
                 block = block - factor_col * top
-            r_ref[pl.ds(r0, GROUP), base:] = rows[:, :n - base]
-            x_ref[pl.ds(r0, GROUP), :] = rows[:, n - base:]
-            head = jnp.transpose(rows[:, :PANEL])
-            for t in range(GROUP):
-                row_ref[t, :, :span] = jnp.broadcast_to(rows[t:t + 1, :], (GROUP, span))
-                head_ref[t] = jnp.broadcast_to(head[:, t:t + 1], (PANEL, PANEL))
-
-            def slab(s, c):
-                at = pl.multiple_of(base + s * GROUP, GROUP)
-                off = pl.multiple_of(s * GROUP, GROUP)
-                part = w_ref[pl.ds(at, GROUP), base:]
+            r_ref[r0:r0 + GROUP, base:] = rows[:, :n - base]
+            x_ref[r0:r0 + GROUP, :] = rows[:, n - base:]
+            below = r0 + GROUP - base
+            if below < PANEL:
+                head = jnp.transpose(rows[:, :PANEL])
                 for t in range(GROUP):
-                    mult = head_ref[t, pl.ds(off, GROUP), :]
-                    mult = jnp.concatenate([mult] * (span // PANEL), axis=1)
-                    part = part - mult * row_ref[t, :, :span]
-                w_ref[pl.ds(at, GROUP), base:] = part
-                return c
-
-            lax.fori_loop(g + 1, PANEL // GROUP, slab, 0)
-            return carry
-
-        lax.fori_loop(0, PANEL // GROUP, group, 0)
+                    row_ref[t, :, :span] = jnp.broadcast_to(rows[t:t + 1, :], (GROUP, span))
+                    head_ref[t, below:, :] = jnp.broadcast_to(head[below:, t:t + 1], (PANEL - below, PANEL))
+                for at in range(below, PANEL, GROUP):
+                    part = w_ref[base + at:base + at + GROUP, base:]
+                    for t in range(GROUP):
+                        mult = head_ref[t, at:at + GROUP, :]
+                        mult = jnp.concatenate([mult] * (span // PANEL), axis=1)
+                        part = part - mult * row_ref[t, :, :span]
+                    w_ref[base + at:base + at + GROUP, base:] = part
         rest = base + PANEL
         if rest < n:
             left = r_ref[base:rest, rest:]
@@ -117,9 +104,9 @@
     width = k // n_col
     col = lax.axis_index("col")
     columns = lax.dynamic_slice_in_dim(sketch, col * width, width, 1)
-    gram_part = jnp.dot(sketch.T, columns, precision=lax.Precision.HIGHEST)
+    gram_part = jnp.dot(sketch.T, columns, precision=lax.Precision.HIGHEST) / jnp.float32(total_rows)
     gram_part = gather_rows(scatter_sum(gram_part, "row", n_row), "row", n_row)
-    gram = gather_rows(gram_part.T, "col", n_col) / jnp.float32(total_rows)
+    gram = gather_rows(gram_part.T, "col", n_col)
     share = own_rows.shape[0]
     extra = jnp.concatenate([own_rows.T, jnp.zeros((k, PANEL - share), jnp.float32)], axis=1)
     upper, solved = factor(gram, extra)

time: 282 us -> 262 us (0.929)
  Pallas kernels: 68.6 us -> 49.1 us
    pallas_call x1, Pallas kernels: 68.6 us -> 49.1 us  [factor(): pl.pallas_call(factor_kernel, out_shape=(jax.ShapeDtypeStruct((n, n), jnp...]
where the time goes in v7:
time: 262 us; the launch traced here: 259 us
  waiting for transfers between devices  126 us (48%)
  Pallas kernels  49.1 us (19%)
  blocking collectives  40 us (15%)
  between operations  14.1 us (5%)
  matrix products  11 us (4%)
  starting transfers between devices  9.72 us (4%)
  local copies, waits for them, and re-layouts  7.07 us (3%)
    all_gather x1, waiting for transfers between devices, probe_product(): lax.all_gather(test_matrix, 'row', axis=0, tiled=True)  100 us
    pallas_call x1, Pallas kernels, factor(): pl.pallas_call(factor_kernel, out_shape=(jax.ShapeDtypeStruct((n, n), jnp...  49.1 us
    all_to_all x2, blocking collectives, scatter_sum(): return lax.all_to_all(pieces, axis, 0, 0, tiled=False).sum(0)  29.6 us
    all_to_all x2, waiting for transfers between devices, gather_rows(): gathered = lax.all_to_all(copies, axis, 0, 0, tiled=False)  25.4 us
    dot_general x1, matrix products, probe_product(): jnp.dot(matrix, lax.all_gather(test_matrix, 'row', axis=0, tiled=True), p...  10.5 us
    all_to_all x1, blocking collectives, gather_rows(): gathered = lax.all_to_all(copies, axis, 0, 0, tiled=False)  10.4 us
    all_to_all x2, starting transfers between devices, gather_rows(): gathered = lax.all_to_all(copies, axis, 0, 0, tiled=False)  9.68 us
  transfers between devices with their start and end apart: 3, of which 3 were waited for; matrix products, arithmetic and copies ran while one was open for 0% of the time, Pallas kernels for 0%

profile of v7, /device:TPU:2, one launch (start us, length us, event | category | flops | bytes accessed | tf_op | source)
XLA Modules:
  0.0 259.0 jit_solution(17920287849383205437)
XLA Ops:
  7.2 0.0 all-gather.2.cloned.1.call-start
  7.2 0.7 all-gather.2.cloned.1.call-update
  7.9 100.2 %all-gather.2.cloned.1.call-done = bf16[16384,512]{1,0:T(8,128)(2,1)} async-done(((bf16[1024,512]{1,0:T(8,128)(2,1)}), bf16[16384,512]{1,0:T(8,128)(2,1)}) %all-gather.2.cloned.1.call-update) | async-done | bytes 16777232 | tf_op jit(solution)/shard_map/all_gather | solution.py:80
  108.1 10.5 %fusion.2 = f32[256,512]{1,0:T(8,128)S(1)} fusion(bf16[256,16384]{1,0:T(8,128)(2,1)} %param.2, bf16[16384,512]{1,0:T(8,128)(2,1)} %all-gather.2.cloned.1.call-done), kind=kOutput, calls=%fused_computation.7 | convolution fusion | flops 4294967296 | bytes 25690112 | tf_op jit(solution)/shard_map/dot_general | solution.py:78
  118.6 17.7 %all_to_all.25 = f32[16,16,512]{2,1,0:T(8,128)S(1)} all-to-all(f32[16,16,512]{2,1,0:T(8,128)S(1)} %bitcast.27), channel_id=1, replica_groups=mesh['row'=16,'col'=16] {'col'}, dimensions={0} | all-to-all | bytes 1048576 | tf_op jit(solution)/shard_map/all_to_all | solution.py:87
  136.3 0.9 broadcast_in_dim.6
  137.2 4.8 %all-to-all-start.1 = ((f32[16,16,512]{2,1,0:T(8,128)}), f32[16,16,512]{2,1,0:T(8,128)S(1)}, u32[]{:S(2)}, u32[]{:S(2)}) async-start(f32[16,16,512]{2,1,0:T(8,128)} %broadcast_in_dim.6), calls=%async_computation.1 | async-start | bytes 1048576 | tf_op jit(solution)/shard_map/all_to_all | solution.py:92
  142.0 9.6 %all-to-all-done.1 = f32[16,16,512]{2,1,0:T(8,128)S(1)} async-done(((f32[16,16,512]{2,1,0:T(8,128)}), f32[16,16,512]{2,1,0:T(8,128)S(1)}, u32[]{:S(2)}, u32[]{:S(2)}) %all-to-all-start.1) | async-done | bytes 524320 | tf_op jit(solution)/shard_map/all_to_all | solution.py:92
  151.6 0.5 convolution_multiply_fusion
  152.1 0.1 reshape.24
  152.2 0.1 copy.14
  152.3 0.2 reshape.27
  152.5 12.0 %all_to_all.26 = f32[16,1,1024]{2,1,0:T(1,128)S(1)} all-to-all(f32[16,1,1024]{2,1,0:T(1,128)S(1)} %reshape.27), channel_id=1, replica_groups=mesh['row'=16,'col'=16] {'row'}, dimensions={0} | all-to-all | bytes 131072 | tf_op jit(solution)/shard_map/all_to_all | solution.py:87
  164.4 0.5 broadcast.6
  164.9 0.8 reduce
  165.7 0.1 reshape.28
  165.9 0.2 reshape.29
  166.1 10.4 %all_to_all.27 = f32[16,1,1024]{2,1,0:T(1,128)S(1)} all-to-all(f32[16,1,1024]{2,1,0:T(1,128)S(1)} %reshape.29), channel_id=1, replica_groups=mesh['row'=16,'col'=16] {'row'}, dimensions={0} | all-to-all | bytes 131072 | tf_op jit(solution)/shard_map/all_to_all | solution.py:92
  176.5 0.8 reduce.1
  177.3 0.1 reshape.30
  177.4 0.2 copy.10
  177.6 0.1 reshape.25
  177.7 1.1 broadcast_in_dim.8
  178.8 4.9 %all-to-all-start.4 = ((f32[16,32,512]{2,1,0:T(8,128)}), f32[16,32,512]{2,1,0:T(8,128)S(1)}, u32[]{:S(2)}, u32[]{:S(2)}) async-start(f32[16,32,512]{2,1,0:T(8,128)} %broadcast_in_dim.8), calls=%async_computation.4 | async-start | bytes 2097152 | tf_op jit(solution)/shard_map/all_to_all | solution.py:92
  183.6 0.1 copy.11
  183.8 0.7 concatenate.3.e_ref
  184.5 15.8 %all-to-all-done.4 = f32[16,32,512]{2,1,0:T(8,128)S(1)} async-done(((f32[16,32,512]{2,1,0:T(8,128)}), f32[16,32,512]{2,1,0:T(8,128)S(1)}, u32[]{:S(2)}, u32[]{:S(2)}) %all-to-all-start.4) | async-done | bytes 1048608 | tf_op jit(solution)/shard_map/all_to_all | solution.py:92
  200.4 0.0 copy-start
  200.4 1.0 copy-done
  201.3 49.1 %shard_map.41 = (f32[512,512]{1,0:T(8,128)}, f32[512,128]{1,0:T(8,128)}) custom-call(f32[512,512]{1,0:T(8,128)} %bitcast.22, f32[512,128]{1,0:T(8,128)} %concatenate.3.e_ref), custom_call_target="tpu_custom_call" | custom-call | tf_op jit(solution)/shard_map/pallas_call | solution.py:64
  250.4 1.0 slice_bitcast_fusion
  251.4 0.7 copy.12
  (3 shorter events, 0.1 us)
Async XLA Ops:
  7.2 101.0 %all-gather.2.cloned.1.call-start = ((), (), s32[]{:S(2)}) async-start(), calls=%async_computation.5 | async-start | bytes 17825792 | tf_op jit(solution)/shard_map/all_gather | solution.py:80
  137.2 14.4 %all-to-all-start.1 = ((f32[16,16,512]{2,1,0:T(8,128)}), f32[16,16,512]{2,1,0:T(8,128)S(1)}, u32[]{:S(2)}, u32[]{:S(2)}) async-start(f32[16,16,512]{2,1,0:T(8,128)} %broadcast_in_dim.6), calls=%async_computation.1 | async-start | bytes 1048576 | tf_op jit(solution)/shard_map/all_to_all | solution.py:92
  178.8 21.6 %all-to-all-start.4 = ((f32[16,32,512]{2,1,0:T(8,128)}), f32[16,32,512]{2,1,0:T(8,128)S(1)}, u32[]{:S(2)}, u32[]{:S(2)}) async-start(f32[16,32,512]{2,1,0:T(8,128)} %broadcast_in_dim.8), calls=%async_computation.4 | async-start | bytes 2097152 | tf_op jit(solution)/shard_map/all_to_all | solution.py:92
  200.4 1.0 copy-start
Sparse Core Ops, SparseCore 0:
  9.8 98.2 all-gather.1

commit v8 on v7

--- a/solution.py
+++ b/solution.py
@@ -93,6 +93,15 @@
     return gathered.reshape(parts * value.shape[0], *value.shape[1:])
 
 
+def butterfly_sum(value, axis, parts):
+    assert parts & (parts - 1) == 0
+    distance = 1
+    while distance < parts:
+        value = value + lax.ppermute(value, axis, [(i, i ^ distance) for i in range(parts)])
+        distance *= 2
+    return value
+
+
 def shards(matrix, test_matrix):
     n_col = lax.axis_size("col")
     n_row = lax.axis_size("row")
@@ -105,7 +114,7 @@
     col = lax.axis_index("col")
     columns = lax.dynamic_slice_in_dim(sketch, col * width, width, 1)
     gram_part = jnp.dot(sketch.T, columns, precision=lax.Precision.HIGHEST) / jnp.float32(total_rows)
-    gram_part = gather_rows(scatter_sum(gram_part, "row", n_row), "row", n_row)
+    gram_part = butterfly_sum(gram_part, "row", n_row)
     gram = gather_rows(gram_part.T, "col", n_col)
     share = own_rows.shape[0]
     extra = jnp.concatenate([own_rows.T, jnp.zeros((k, PANEL - share), jnp.float32)], axis=1)

time: 262 us -> 251 us (0.958)
  blocking collectives: 40 us -> 17.7 us
  waiting for transfers between devices: 126 us -> 139 us
  starting transfers between devices: 9.72 us -> 13.9 us
    ppermute x0 -> x4, waiting for transfers between devices: none -> 15.6 us  [butterfly_sum(): lax.ppermute(value, axis, [(i, i ^ distance) for i in range(parts)])]
    all_to_all x2 -> x1, blocking collectives: 29.6 us -> 17.7 us  [scatter_sum(): return lax.all_to_all(pieces, axis, 0, 0, tiled=False).sum(0)]
    all_to_all x1 -> x0, blocking collectives: 10.4 us -> none  [gather_rows(): gathered = lax.all_to_all(copies, axis, 0, 0, tiled=False)]
    ppermute x0 -> x4, starting transfers between devices: none -> 4.19 us  [butterfly_sum(): lax.ppermute(value, axis, [(i, i ^ distance) for i in range(parts)])]
    all_to_all x2, waiting for transfers between devices: 25.4 us -> 22.5 us  [gather_rows(): gathered = lax.all_to_all(copies, axis, 0, 0, tiled=False)]
  transfers between devices with their start and end apart: 3 -> 7, of which waited for: 3 -> 7; matrix products, arithmetic and copies ran while one was open for 0% -> 0% of each run, Pallas kernels for 0% -> 0%
where the time goes in v8:
time: 251 us; the launch traced here: 250 us
  waiting for transfers between devices  139 us (55%)
  Pallas kernels  49.1 us (20%)
  blocking collectives  17.7 us (7%)
  between operations  14.1 us (6%)
  starting transfers between devices  13.9 us (6%)
  matrix products  11 us (4%)
  local copies, waits for them, and re-layouts  5.47 us (2%)
    all_gather x1, waiting for transfers between devices, probe_product(): lax.all_gather(test_matrix, 'row', axis=0, tiled=True)  100 us
    pallas_call x1, Pallas kernels, factor(): pl.pallas_call(factor_kernel, out_shape=(jax.ShapeDtypeStruct((n, n), jnp...  49.1 us
    all_to_all x2, waiting for transfers between devices, gather_rows(): gathered = lax.all_to_all(copies, axis, 0, 0, tiled=False)  22.5 us
    all_to_all x1, blocking collectives, scatter_sum(): return lax.all_to_all(pieces, axis, 0, 0, tiled=False).sum(0)  17.7 us
    ppermute x4, waiting for transfers between devices, butterfly_sum(): lax.ppermute(value, axis, [(i, i ^ distance) for i in range(parts)])  15.6 us
    dot_general x1, matrix products, probe_product(): jnp.dot(matrix, lax.all_gather(test_matrix, 'row', axis=0, tiled=True), p...  10.5 us
    all_to_all x2, starting transfers between devices, gather_rows(): gathered = lax.all_to_all(copies, axis, 0, 0, tiled=False)  9.68 us
  transfers between devices with their start and end apart: 7, of which 7 were waited for; matrix products, arithmetic and copies ran while one was open for 0% of the time, Pallas kernels for 0%

profile of v8, /device:TPU:2, one launch (start us, length us, event | category | flops | bytes accessed | tf_op | source)
XLA Modules:
  0.0 250.2 jit_solution(15252080700248112699)
XLA Ops:
  7.2 0.0 all-gather.2.cloned.1.call-start
  7.2 0.7 all-gather.2.cloned.1.call-update
  7.9 100.2 %all-gather.2.cloned.1.call-done = bf16[16384,512]{1,0:T(8,128)(2,1)} async-done(((bf16[1024,512]{1,0:T(8,128)(2,1)}), bf16[16384,512]{1,0:T(8,128)(2,1)}) %all-gather.2.cloned.1.call-update) | async-done | bytes 16777232 | tf_op jit(solution)/shard_map/all_gather | solution.py:80
  108.1 10.5 %fusion.2 = f32[256,512]{1,0:T(8,128)S(1)} fusion(bf16[256,16384]{1,0:T(8,128)(2,1)} %param.2, bf16[16384,512]{1,0:T(8,128)(2,1)} %all-gather.2.cloned.1.call-done), kind=kOutput, calls=%fused_computation.5 | convolution fusion | flops 4294967296 | bytes 25690112 | tf_op jit(solution)/shard_map/dot_general | solution.py:78
  118.6 17.7 %all_to_all.15 = f32[16,16,512]{2,1,0:T(8,128)S(1)} all-to-all(f32[16,16,512]{2,1,0:T(8,128)S(1)} %bitcast.14), channel_id=1, replica_groups=mesh['row'=16,'col'=16] {'col'}, dimensions={0} | all-to-all | bytes 1048576 | tf_op jit(solution)/shard_map/all_to_all | solution.py:87
  136.3 0.9 broadcast_in_dim.4
  137.2 4.8 %all-to-all-start.1 = ((f32[16,16,512]{2,1,0:T(8,128)}), f32[16,16,512]{2,1,0:T(8,128)S(1)}, u32[]{:S(2)}, u32[]{:S(2)}) async-start(f32[16,16,512]{2,1,0:T(8,128)} %broadcast_in_dim.4), calls=%async_computation.1 | async-start | bytes 1048576 | tf_op jit(solution)/shard_map/all_to_all | solution.py:92
  142.0 9.6 %all-to-all-done.1 = f32[16,16,512]{2,1,0:T(8,128)S(1)} async-done(((f32[16,16,512]{2,1,0:T(8,128)}), f32[16,16,512]{2,1,0:T(8,128)S(1)}, u32[]{:S(2)}, u32[]{:S(2)}) %all-to-all-start.1) | async-done | bytes 524320 | tf_op jit(solution)/shard_map/all_to_all | solution.py:92
  151.6 0.5 convolution_multiply_fusion
  152.1 0.1 collective-permute-start
  152.2 1.2 collective-permute-done
  153.4 0.1 collective-permute-start.1
  153.5 4.3 %collective-permute-done.1 = f32[512,32]{0,1:T(8,128)S(1)} collective-permute-done((f32[512,32]{0,1:T(8,128)S(1)}, f32[512,32]{0,1:T(8,128)S(1)}, u32[]{:S(2)}, u32[]{:S(2)}) %collective-permute-start.1) | collective-permute-done | bytes 65568 | tf_op jit(solution)/shard_map/ppermute | solution.py:100
  157.8 1.6 collective-permute-start.2
  159.4 4.2 %collective-permute-done.2 = f32[512,32]{0,1:T(8,128)S(1)} collective-permute-done((f32[512,32]{0,1:T(8,128)S(1)}, f32[512,32]{0,1:T(8,128)S(1)}, u32[]{:S(2)}, u32[]{:S(2)}) %collective-permute-start.2) | collective-permute-done | bytes 65568 | tf_op jit(solution)/shard_map/ppermute | solution.py:100
  163.6 2.4 collective-permute-start.3
  166.0 5.9 %collective-permute-done.3 = f32[512,32]{0,1:T(8,128)S(1)} collective-permute-done((f32[512,32]{0,1:T(8,128)S(1)}, f32[512,32]{0,1:T(8,128)S(1)}, u32[]{:S(2)}, u32[]{:S(2)}) %collective-permute-start.3) | collective-permute-done | bytes 65568 | tf_op jit(solution)/shard_map/ppermute | solution.py:100
  171.9 1.1 broadcast_in_dim.5
  173.0 4.9 %all-to-all-start.2 = ((f32[16,32,512]{2,1,0:T(8,128)}), f32[16,32,512]{2,1,0:T(8,128)S(1)}, u32[]{:S(2)}, u32[]{:S(2)}) async-start(f32[16,32,512]{2,1,0:T(8,128)} %broadcast_in_dim.5), calls=%async_computation.2 | async-start | bytes 2097152 | tf_op jit(solution)/shard_map/all_to_all | solution.py:92
  177.9 0.1 copy.6
  178.0 0.7 concatenate.3.e_ref
  178.7 12.9 %all-to-all-done.2 = f32[16,32,512]{2,1,0:T(8,128)S(1)} async-done(((f32[16,32,512]{2,1,0:T(8,128)}), f32[16,32,512]{2,1,0:T(8,128)S(1)}, u32[]{:S(2)}, u32[]{:S(2)}) %all-to-all-start.2) | async-done | bytes 1048608 | tf_op jit(solution)/shard_map/all_to_all | solution.py:92
  191.6 0.0 copy-start
  191.6 1.0 copy-done
  192.6 49.1 %shard_map.41 = (f32[512,512]{1,0:T(8,128)}, f32[512,128]{1,0:T(8,128)}) custom-call(f32[512,512]{1,0:T(8,128)} %bitcast.11, f32[512,128]{1,0:T(8,128)} %concatenate.3.e_ref), custom_call_target="tpu_custom_call" | custom-call | tf_op jit(solution)/shard_map/pallas_call | solution.py:64
  241.7 1.0 slice_bitcast_fusion
  242.6 0.7 copy.7
  (5 shorter events, 0.1 us)
Async XLA Ops:
  7.2 101.0 %all-gather.2.cloned.1.call-start = ((), (), s32[]{:S(2)}) async-start(), calls=%async_computation.3 | async-start | bytes 17825792 | tf_op jit(solution)/shard_map/all_gather | solution.py:80
  137.2 14.4 %all-to-all-start.1 = ((f32[16,16,512]{2,1,0:T(8,128)}), f32[16,16,512]{2,1,0:T(8,128)S(1)}, u32[]{:S(2)}, u32[]{:S(2)}) async-start(f32[16,16,512]{2,1,0:T(8,128)} %broadcast_in_dim.4), calls=%async_computation.1 | async-start | bytes 1048576 | tf_op jit(solution)/shard_map/all_to_all | solution.py:92
  152.1 1.3 collective-permute-start
  153.4 4.4 %collective-permute-start.1 = (f32[512,32]{0,1:T(8,128)S(1)}, f32[512,32]{0,1:T(8,128)S(1)}, u32[]{:S(2)}, u32[]{:S(2)}) collective-permute-start(f32[512,32]{0,1:T(8,128)S(1)} %add.18), channel_id=1, source_target_pairs={{0,32},{16,48},{32,0},{48,16},{64,96},{80,112},{96,64},{112,80},{1... | collective-permute-start | bytes 196616 | tf_op jit(solution)/shard_map/ppermute | solution.py:100
  157.8 5.8 %collective-permute-start.2 = (f32[512,32]{0,1:T(8,128)S(1)}, f32[512,32]{0,1:T(8,128)S(1)}, u32[]{:S(2)}, u32[]{:S(2)}) collective-permute-start(f32[512,32]{0,1:T(8,128)S(1)} %add.19), channel_id=1, source_target_pairs={{0,64},{16,80},{32,96},{48,112},{64,0},{80,16},{96,32},{112,48},{1... | collective-permute-start | bytes 196616 | tf_op jit(solution)/shard_map/ppermute | solution.py:100
  163.6 8.3 %collective-permute-start.3 = (f32[512,32]{0,1:T(8,128)S(1)}, f32[512,32]{0,1:T(8,128)S(1)}, u32[]{:S(2)}, u32[]{:S(2)}) collective-permute-start(f32[512,32]{0,1:T(8,128)S(1)} %add.20), channel_id=1, source_target_pairs={{0,128},{16,144},{32,160},{48,176},{64,192},{80,208},{96,224},{112... | collective-permute-start | bytes 196616 | tf_op jit(solution)/shard_map/ppermute | solution.py:100
  173.0 18.6 %all-to-all-start.2 = ((f32[16,32,512]{2,1,0:T(8,128)}), f32[16,32,512]{2,1,0:T(8,128)S(1)}, u32[]{:S(2)}, u32[]{:S(2)}) async-start(f32[16,32,512]{2,1,0:T(8,128)} %broadcast_in_dim.5), calls=%async_computation.2 | async-start | bytes 2097152 | tf_op jit(solution)/shard_map/all_to_all | solution.py:92
  191.6 1.0 copy-start
Sparse Core Ops, SparseCore 0:
  9.8 98.2 all-gather.1

commit v9 on v8

--- a/solution.py
+++ b/solution.py
@@ -114,8 +114,10 @@
     col = lax.axis_index("col")
     columns = lax.dynamic_slice_in_dim(sketch, col * width, width, 1)
     gram_part = jnp.dot(sketch.T, columns, precision=lax.Precision.HIGHEST) / jnp.float32(total_rows)
-    gram_part = butterfly_sum(gram_part, "row", n_row)
-    gram = gather_rows(gram_part.T, "col", n_col)
+    half = k // 2
+    gram = jnp.concatenate(
+        [gather_rows(butterfly_sum(gram_part[h:h + half], "row", n_row).T, "col", n_col) for h in (0, half)], axis=1
+    )
     share = own_rows.shape[0]
     extra = jnp.concatenate([own_rows.T, jnp.zeros((k, PANEL - share), jnp.float32)], axis=1)
     upper, solved = factor(gram, extra)

time: 251 us -> 270 us (1.076)
  starting transfers between devices: 13.9 us -> 25.5 us
  waiting for transfers between devices: 139 us -> 145 us
    ppermute x4 -> x8, waiting for transfers between devices: 15.6 us -> 27 us  [butterfly_sum(): lax.ppermute(value, axis, [(i, i ^ distance) for i in range(parts)])]
    all_to_all x2 -> x3, starting transfers between devices: 9.68 us -> 17.1 us  [gather_rows(): gathered = lax.all_to_all(copies, axis, 0, 0, tiled=False)]
    all_to_all x2 -> x3, waiting for transfers between devices: 22.5 us -> 17.5 us  [gather_rows(): gathered = lax.all_to_all(copies, axis, 0, 0, tiled=False)]
    ppermute x4 -> x8, starting transfers between devices: 4.19 us -> 8.31 us  [butterfly_sum(): lax.ppermute(value, axis, [(i, i ^ distance) for i in range(parts)])]
  transfers between devices with their start and end apart: 7 -> 12, of which waited for: 7 -> 11; matrix products, arithmetic and copies ran while one was open for 0% -> 0% of each run, Pallas kernels for 0% -> 0%
where the time goes in v9:
time: 270 us; the launch traced here: 269 us
  waiting for transfers between devices  145 us (54%)
  Pallas kernels  49.1 us (18%)
  starting transfers between devices  25.5 us (9%)
  blocking collectives  17.7 us (7%)
  between operations  14.1 us (5%)
  matrix products  11 us (4%)
  local copies, waits for them, and re-layouts  5.1 us (2%)
    all_gather x1, waiting for transfers between devices, probe_product(): lax.all_gather(test_matrix, 'row', axis=0, tiled=True)  100 us
    pallas_call x1, Pallas kernels, factor(): pl.pallas_call(factor_kernel, out_shape=(jax.ShapeDtypeStruct((n, n), jnp...  49.1 us
    ppermute x8, waiting for transfers between devices, butterfly_sum(): lax.ppermute(value, axis, [(i, i ^ distance) for i in range(parts)])  27 us
    all_to_all x1, blocking collectives, scatter_sum(): return lax.all_to_all(pieces, axis, 0, 0, tiled=False).sum(0)  17.7 us
    all_to_all x3, waiting for transfers between devices, gather_rows(): gathered = lax.all_to_all(copies, axis, 0, 0, tiled=False)  17.5 us
    all_to_all x3, starting transfers between devices, gather_rows(): gathered = lax.all_to_all(copies, axis, 0, 0, tiled=False)  17.1 us
    dot_general x1, matrix products, probe_product(): jnp.dot(matrix, lax.all_gather(test_matrix, 'row', axis=0, tiled=True), p...  10.5 us
    ppermute x8, starting transfers between devices, butterfly_sum(): lax.ppermute(value, axis, [(i, i ^ distance) for i in range(parts)])  8.31 us
  transfers between devices with their start and end apart: 12, of which 11 were waited for; matrix products, arithmetic and copies ran while one was open for 0% of the time, Pallas kernels for 0%

profile of v9, /device:TPU:2, one launch (start us, length us, event | category | flops | bytes accessed | tf_op | source)
XLA Modules:
  0.0 269.0 jit_solution(2781321977093658753)
XLA Ops:
  7.2 0.0 all-gather.2.cloned.1.call-start
  7.2 0.7 all-gather.2.cloned.1.call-update
  7.9 100.2 %all-gather.2.cloned.1.call-done = bf16[16384,512]{1,0:T(8,128)(2,1)} async-done(((bf16[1024,512]{1,0:T(8,128)(2,1)}), bf16[16384,512]{1,0:T(8,128)(2,1)}) %all-gather.2.cloned.1.call-update) | async-done | bytes 16777232 | tf_op jit(solution)/shard_map/all_gather | solution.py:80
  108.1 10.5 %fusion.3 = f32[256,512]{1,0:T(8,128)S(1)} fusion(bf16[256,16384]{1,0:T(8,128)(2,1)} %param.2, bf16[16384,512]{1,0:T(8,128)(2,1)} %all-gather.2.cloned.1.call-done), kind=kOutput, calls=%fused_computation.10 | convolution fusion | flops 4294967296 | bytes 25690112 | tf_op jit(solution)/shard_map/dot_general | solution.py:78
  118.6 17.7 %all_to_all.20 = f32[16,16,512]{2,1,0:T(8,128)S(1)} all-to-all(f32[16,16,512]{2,1,0:T(8,128)S(1)} %bitcast.18), channel_id=1, replica_groups=mesh['row'=16,'col'=16] {'col'}, dimensions={0} | all-to-all | bytes 1048576 | tf_op jit(solution)/shard_map/all_to_all | solution.py:87
  136.3 0.9 broadcast_in_dim.6
  137.2 4.8 %all-to-all-start.1 = ((f32[16,16,512]{2,1,0:T(8,128)}), f32[16,16,512]{2,1,0:T(8,128)S(1)}, u32[]{:S(2)}, u32[]{:S(2)}) async-start(f32[16,16,512]{2,1,0:T(8,128)} %broadcast_in_dim.6), calls=%async_computation.1 | async-start | bytes 1048576 | tf_op jit(solution)/shard_map/all_to_all | solution.py:92
  142.0 9.6 %all-to-all-done.1 = f32[16,16,512]{2,1,0:T(8,128)S(1)} async-done(((f32[16,16,512]{2,1,0:T(8,128)}), f32[16,16,512]{2,1,0:T(8,128)S(1)}, u32[]{:S(2)}, u32[]{:S(2)}) %all-to-all-start.1) | async-done | bytes 524320 | tf_op jit(solution)/shard_map/all_to_all | solution.py:92
  151.6 0.5 convolution_multiply_fusion
  152.1 0.1 collective-permute-start
  152.2 0.5 collective-permute-start.4
  152.7 0.7 collective-permute-done
  153.4 0.2 collective-permute-done.4
  153.6 0.1 collective-permute-start.5
  153.7 3.9 %collective-permute-done.5 = f32[256,32]{0,1:T(8,128)S(1)} collective-permute-done((f32[256,32]{0,1:T(8,128)S(1)}, f32[256,32]{0,1:T(8,128)S(1)}, u32[]{:S(2)}, u32[]{:S(2)}) %collective-permute-start.5) | collective-permute-done | bytes 32800 | tf_op jit(solution)/shard_map/ppermute | solution.py:100
  157.6 1.4 collective-permute-start.6
  158.9 3.7 %collective-permute-done.6 = f32[256,32]{0,1:T(8,128)S(1)} collective-permute-done((f32[256,32]{0,1:T(8,128)S(1)}, f32[256,32]{0,1:T(8,128)S(1)}, u32[]{:S(2)}, u32[]{:S(2)}) %collective-permute-start.6) | collective-permute-done | bytes 32800 | tf_op jit(solution)/shard_map/ppermute | solution.py:100
  162.6 2.7 collective-permute-start.7
  165.3 5.2 %collective-permute-done.7 = f32[256,32]{0,1:T(8,128)S(1)} collective-permute-done((f32[256,32]{0,1:T(8,128)S(1)}, f32[256,32]{0,1:T(8,128)S(1)}, u32[]{:S(2)}, u32[]{:S(2)}) %collective-permute-start.7) | collective-permute-done | bytes 32800 | tf_op jit(solution)/shard_map/ppermute | solution.py:100
  170.4 0.8 broadcast_in_dim.8
  171.3 4.8 %all-to-all-start.3 = ((f32[16,32,256]{2,1,0:T(8,128)}), f32[16,32,256]{2,1,0:T(8,128)S(1)}, u32[]{:S(2)}, u32[]{:S(2)}) async-start(f32[16,32,256]{2,1,0:T(8,128)} %broadcast_in_dim.8), calls=%async_computation.3 | async-start | bytes 1048576 | tf_op jit(solution)/shard_map/all_to_all | solution.py:92
  176.1 0.4 collective-permute-start.1
  176.4 3.6 %collective-permute-done.1 = f32[256,32]{0,1:T(8,128)S(1)} collective-permute-done((f32[256,32]{0,1:T(8,128)S(1)}, f32[256,32]{0,1:T(8,128)S(1)}, u32[]{:S(2)}, u32[]{:S(2)}) %collective-permute-start.1) | collective-permute-done | bytes 32800 | tf_op jit(solution)/shard_map/ppermute | solution.py:100
  180.1 1.0 collective-permute-start.2
  181.1 4.1 %collective-permute-done.2 = f32[256,32]{0,1:T(8,128)S(1)} collective-permute-done((f32[256,32]{0,1:T(8,128)S(1)}, f32[256,32]{0,1:T(8,128)S(1)}, u32[]{:S(2)}, u32[]{:S(2)}) %collective-permute-start.2) | collective-permute-done | bytes 32800 | tf_op jit(solution)/shard_map/ppermute | solution.py:100
  185.3 2.2 collective-permute-start.3
  187.5 5.6 %collective-permute-done.3 = f32[256,32]{0,1:T(8,128)S(1)} collective-permute-done((f32[256,32]{0,1:T(8,128)S(1)}, f32[256,32]{0,1:T(8,128)S(1)}, u32[]{:S(2)}, u32[]{:S(2)}) %collective-permute-start.3) | collective-permute-done | bytes 32800 | tf_op jit(solution)/shard_map/ppermute | solution.py:100
  193.1 0.0 all-to-all-done.3
  193.1 0.8 broadcast_in_dim.7
  193.9 7.5 %all-to-all-start.2 = ((f32[16,32,256]{2,1,0:T(8,128)}), f32[16,32,256]{2,1,0:T(8,128)S(1)}, u32[]{:S(2)}, u32[]{:S(2)}) async-start(f32[16,32,256]{2,1,0:T(8,128)} %broadcast_in_dim.7), calls=%async_computation.2 | async-start | bytes 1048576 | tf_op jit(solution)/shard_map/all_to_all | solution.py:92
  201.5 0.1 copy.6
  201.6 0.7 concatenate.7.e_ref
  202.4 7.9 %all-to-all-done.2 = f32[16,32,256]{2,1,0:T(8,128)S(1)} async-done(((f32[16,32,256]{2,1,0:T(8,128)}), f32[16,32,256]{2,1,0:T(8,128)S(1)}, u32[]{:S(2)}, u32[]{:S(2)}) %all-to-all-start.2) | async-done | bytes 524320 | tf_op jit(solution)/shard_map/all_to_all | solution.py:92
  210.3 1.1 pad_maximum_fusion.a_ref
  211.4 49.1 %shard_map.41 = (f32[512,512]{1,0:T(8,128)}, f32[512,128]{1,0:T(8,128)}) custom-call(f32[512,512]{1,0:T(8,128)} %pad_maximum_fusion.a_ref, f32[512,128]{1,0:T(8,128)} %concatenate.7.e_ref), custom_call_target="tpu_custom_call" | custom-call | tf_op jit(solution)/shard_map/pallas_call | solution.py:64
  260.5 1.0 slice_bitcast_fusion
  261.5 0.7 copy.7
  (9 shorter events, 0.1 us)
Async XLA Ops:
  7.2 101.0 %all-gather.2.cloned.1.call-start = ((), (), s32[]{:S(2)}) async-start(), calls=%async_computation.4 | async-start | bytes 17825792 | tf_op jit(solution)/shard_map/all_gather | solution.py:80
  137.2 14.4 %all-to-all-start.1 = ((f32[16,16,512]{2,1,0:T(8,128)}), f32[16,16,512]{2,1,0:T(8,128)S(1)}, u32[]{:S(2)}, u32[]{:S(2)}) async-start(f32[16,16,512]{2,1,0:T(8,128)} %broadcast_in_dim.6), calls=%async_computation.1 | async-start | bytes 1048576 | tf_op jit(solution)/shard_map/all_to_all | solution.py:92
  152.1 1.3 collective-permute-start
  152.2 1.4 collective-permute-start.4
  153.6 4.0 %collective-permute-start.5 = (f32[256,32]{0,1:T(8,128)S(1)}, f32[256,32]{0,1:T(8,128)S(1)}, u32[]{:S(2)}, u32[]{:S(2)}) collective-permute-start(f32[256,32]{0,1:T(8,128)S(1)} %get-tuple-element.11), channel_id=1, source_target_pairs={{0,32},{16,48},{32,0},{48,16},{64,96},{80,112},{96,64},{112,80},{1... | collective-permute-start | bytes 98312 | tf_op jit(solution)/shard_map/ppermute | solution.py:100
  157.6 5.0 %collective-permute-start.6 = (f32[256,32]{0,1:T(8,128)S(1)}, f32[256,32]{0,1:T(8,128)S(1)}, u32[]{:S(2)}, u32[]{:S(2)}) collective-permute-start(f32[256,32]{0,1:T(8,128)S(1)} %add.35), channel_id=1, source_target_pairs={{0,64},{16,80},{32,96},{48,112},{64,0},{80,16},{96,32},{112,48},{1... | collective-permute-start | bytes 98312 | tf_op jit(solution)/shard_map/ppermute | solution.py:100
  162.6 7.8 %collective-permute-start.7 = (f32[256,32]{0,1:T(8,128)S(1)}, f32[256,32]{0,1:T(8,128)S(1)}, u32[]{:S(2)}, u32[]{:S(2)}) collective-permute-start(f32[256,32]{0,1:T(8,128)S(1)} %add.36), channel_id=1, source_target_pairs={{0,128},{16,144},{32,160},{48,176},{64,192},{80,208},{96,224},{112... | collective-permute-start | bytes 98312 | tf_op jit(solution)/shard_map/ppermute | solution.py:100
  171.3 21.8 %all-to-all-start.3 = ((f32[16,32,256]{2,1,0:T(8,128)}), f32[16,32,256]{2,1,0:T(8,128)S(1)}, u32[]{:S(2)}, u32[]{:S(2)}) async-start(f32[16,32,256]{2,1,0:T(8,128)} %broadcast_in_dim.8), calls=%async_computation.3 | async-start | bytes 1048576 | tf_op jit(solution)/shard_map/all_to_all | solution.py:92
  176.1 4.0 %collective-permute-start.1 = (f32[256,32]{0,1:T(8,128)S(1)}, f32[256,32]{0,1:T(8,128)S(1)}, u32[]{:S(2)}, u32[]{:S(2)}) collective-permute-start(f32[256,32]{0,1:T(8,128)S(1)} %get-tuple-element.10), channel_id=1, source_target_pairs={{0,32},{16,48},{32,0},{48,16},{64,96},{80,112},{96,64},{112,80},{1... | collective-permute-start | bytes 98312 | tf_op jit(solution)/shard_map/ppermute | solution.py:100
  180.1 5.2 %collective-permute-start.2 = (f32[256,32]{0,1:T(8,128)S(1)}, f32[256,32]{0,1:T(8,128)S(1)}, u32[]{:S(2)}, u32[]{:S(2)}) collective-permute-start(f32[256,32]{0,1:T(8,128)S(1)} %add.31), channel_id=1, source_target_pairs={{0,64},{16,80},{32,96},{48,112},{64,0},{80,16},{96,32},{112,48},{1... | collective-permute-start | bytes 98312 | tf_op jit(solution)/shard_map/ppermute | solution.py:100
  185.3 7.8 %collective-permute-start.3 = (f32[256,32]{0,1:T(8,128)S(1)}, f32[256,32]{0,1:T(8,128)S(1)}, u32[]{:S(2)}, u32[]{:S(2)}) collective-permute-start(f32[256,32]{0,1:T(8,128)S(1)} %add.32), channel_id=1, source_target_pairs={{0,128},{16,144},{32,160},{48,176},{64,192},{80,208},{96,224},{112... | collective-permute-start | bytes 98312 | tf_op jit(solution)/shard_map/ppermute | solution.py:100
  193.9 16.3 %all-to-all-start.2 = ((f32[16,32,256]{2,1,0:T(8,128)}), f32[16,32,256]{2,1,0:T(8,128)S(1)}, u32[]{:S(2)}, u32[]{:S(2)}) async-start(f32[16,32,256]{2,1,0:T(8,128)} %broadcast_in_dim.7), calls=%async_computation.2 | async-start | bytes 1048576 | tf_op jit(solution)/shard_map/all_to_all | solution.py:92
Sparse Core Ops, SparseCore 0:
  9.8 98.2 all-gather.1

commit v10 on v8

--- a/solution.py
+++ b/solution.py
@@ -9,11 +9,13 @@
 GROUP = 32
 
 
-def factor_kernel(a_ref, e_ref, r_ref, x_ref, w_ref, head_ref, row_ref):
+def factor_kernel(a_ref, e_ref, r_ref, out_ref, x_ref, w_ref, head_ref, row_ref):
     n = a_ref.shape[0]
-    width = n + e_ref.shape[1]
+    width = n + PANEL
+    share = e_ref.shape[0]
     w_ref[:, :n] = a_ref[...]
-    w_ref[:, n:] = e_ref[...]
+    padded = jnp.concatenate([e_ref[...], jnp.zeros((PANEL - share, n), jnp.float32)], axis=0)
+    w_ref[:, n:] = jnp.transpose(padded)
     subl = lax.broadcasted_iota(jnp.int32, (GROUP, 1), 0)
     for k in range(n // PANEL):
         base = k * PANEL
@@ -56,17 +58,19 @@
             left = jnp.transpose(left)
             update = jnp.dot(left, block, precision=lax.Precision.HIGHEST, preferred_element_type=jnp.float32)
             w_ref[rest:n, rest:] = w_ref[rest:n, rest:] - update
+    out_ref[...] = jnp.transpose(x_ref[...])[:share, :]
 
 
 def factor(gram, extra):
-    n, more = gram.shape[0], extra.shape[1]
-    width = n + more
+    n, share = gram.shape[0], extra.shape[0]
+    width = n + PANEL
     return pl.pallas_call(
         factor_kernel,
-        out_shape=(jax.ShapeDtypeStruct((n, n), jnp.float32), jax.ShapeDtypeStruct((n, more), jnp.float32)),
+        out_shape=(jax.ShapeDtypeStruct((n, n), jnp.float32), jax.ShapeDtypeStruct((share, n), jnp.float32)),
         in_specs=[pl.BlockSpec(memory_space=pltpu.VMEM)] * 2,
         out_specs=(pl.BlockSpec(memory_space=pltpu.VMEM),) * 2,
         scratch_shapes=[
+            pltpu.VMEM((n, PANEL), jnp.float32),
             pltpu.VMEM((n, width), jnp.float32),
             pltpu.VMEM((GROUP, PANEL, PANEL), jnp.float32),
             pltpu.VMEM((GROUP, GROUP, width), jnp.float32),
@@ -116,10 +120,8 @@
     gram_part = jnp.dot(sketch.T, columns, precision=lax.Precision.HIGHEST) / jnp.float32(total_rows)
     gram_part = butterfly_sum(gram_part, "row", n_row)
     gram = gather_rows(gram_part.T, "col", n_col)
-    share = own_rows.shape[0]
-    extra = jnp.concatenate([own_rows.T, jnp.zeros((k, PANEL - share), jnp.float32)], axis=1)
-    upper, solved = factor(gram, extra)
-    return (solved[:, :share].T, upper)
+    upper, solved = factor(gram, own_rows)
+    return (solved, upper)
 
 
 def solution(mesh):

time: 251 us -> 246 us (0.980)
  blocking collectives: 17.7 us -> 35.4 us
  waiting for transfers between devices: 139 us -> 126 us
  starting transfers between devices: 13.9 us -> 9.05 us
  local copies, waits for them, and re-layouts: 5.47 us -> 0.97 us
    all_to_all x0 -> x1, blocking collectives: none -> 17.8 us  [gather_rows(): gathered = lax.all_to_all(copies, axis, 0, 0, tiled=False)]
    all_to_all x2 -> x1, waiting for transfers between devices: 22.5 us -> 9.6 us  [gather_rows(): gathered = lax.all_to_all(copies, axis, 0, 0, tiled=False)]
    all_to_all x2 -> x1, starting transfers between devices: 9.68 us -> 4.82 us  [gather_rows(): gathered = lax.all_to_all(copies, axis, 0, 0, tiled=False)]
  transfers between devices with their start and end apart: 7 -> 6, of which waited for: 7 -> 6; matrix products, arithmetic and copies ran while one was open for 0% -> 0% of each run, Pallas kernels for 0% -> 0%
where the time goes in v10:
time: 246 us
  waiting for transfers between devices  126 us (51%)
  Pallas kernels  49.2 us (20%)
  blocking collectives  35.4 us (14%)
  between operations  14.1 us (6%)
  matrix products  11 us (4%)
  starting transfers between devices  9.05 us (4%)
    all_gather x1, waiting for transfers between devices, probe_product(): lax.all_gather(test_matrix, 'row', axis=0, tiled=True)  100 us
    pallas_call x1, Pallas kernels, factor(): pl.pallas_call(factor_kernel, out_shape=(jax.ShapeDtypeStruct((n, n), jnp...  49.2 us
    all_to_all x1, blocking collectives, gather_rows(): gathered = lax.all_to_all(copies, axis, 0, 0, tiled=False)  17.8 us
    all_to_all x1, blocking collectives, scatter_sum(): return lax.all_to_all(pieces, axis, 0, 0, tiled=False).sum(0)  17.7 us
    ppermute x4, waiting for transfers between devices, butterfly_sum(): lax.ppermute(value, axis, [(i, i ^ distance) for i in range(parts)])  15.6 us
    dot_general x1, matrix products, probe_product(): jnp.dot(matrix, lax.all_gather(test_matrix, 'row', axis=0, tiled=True), p...  10.5 us
    all_to_all x1, waiting for transfers between devices, gather_rows(): gathered = lax.all_to_all(copies, axis, 0, 0, tiled=False)  9.6 us
  transfers between devices with their start and end apart: 6, of which 6 were waited for; matrix products, arithmetic and copies ran while one was open for 0% of the time, Pallas kernels for 0%

profile of v10, /device:TPU:2, one launch (start us, length us, event | category | flops | bytes accessed | tf_op | source)
XLA Modules:
  0.0 245.8 jit_solution(1522053789979262500)
XLA Ops:
  7.2 0.0 all-gather.2.cloned.1.call-start
  7.2 0.7 all-gather.2.cloned.1.call-update
  7.9 100.2 %all-gather.2.cloned.1.call-done = bf16[16384,512]{1,0:T(8,128)(2,1)} async-done(((bf16[1024,512]{1,0:T(8,128)(2,1)}), bf16[16384,512]{1,0:T(8,128)(2,1)}) %all-gather.2.cloned.1.call-update) | async-done | bytes 16777232 | tf_op jit(solution)/shard_map/all_gather | solution.py:84
  108.1 10.5 %fusion.2 = f32[256,512]{1,0:T(8,128)S(1)} fusion(bf16[256,16384]{1,0:T(8,128)(2,1)} %param.2, bf16[16384,512]{1,0:T(8,128)(2,1)} %all-gather.2.cloned.1.call-done), kind=kOutput, calls=%fused_computation.4 | convolution fusion | flops 4294967296 | bytes 25690112 | tf_op jit(solution)/shard_map/dot_general | solution.py:82
  118.6 17.7 %all_to_all.15 = f32[16,16,512]{2,1,0:T(8,128)S(1)} all-to-all(f32[16,16,512]{2,1,0:T(8,128)S(1)} %bitcast.10), channel_id=1, replica_groups=mesh['row'=16,'col'=16] {'col'}, dimensions={0} | all-to-all | bytes 1048576 | tf_op jit(solution)/shard_map/all_to_all | solution.py:91
  136.3 0.0 copy-start
  136.3 0.9 broadcast_in_dim.4
  137.2 4.8 %all-to-all-start.1 = ((f32[16,16,512]{2,1,0:T(8,128)}), f32[16,16,512]{2,1,0:T(8,128)S(1)}, u32[]{:S(2)}, u32[]{:S(2)}) async-start(f32[16,16,512]{2,1,0:T(8,128)} %broadcast_in_dim.4), calls=%async_computation.1 | async-start | bytes 1048576 | tf_op jit(solution)/shard_map/all_to_all | solution.py:96
  142.0 9.6 %all-to-all-done.1 = f32[16,16,512]{2,1,0:T(8,128)S(1)} async-done(((f32[16,16,512]{2,1,0:T(8,128)}), f32[16,16,512]{2,1,0:T(8,128)S(1)}, u32[]{:S(2)}, u32[]{:S(2)}) %all-to-all-start.1) | async-done | bytes 524320 | tf_op jit(solution)/shard_map/all_to_all | solution.py:96
  151.6 0.5 convolution_multiply_fusion
  152.1 0.1 collective-permute-start
  152.2 1.2 collective-permute-done
  153.4 0.1 collective-permute-start.1
  153.5 4.3 %collective-permute-done.1 = f32[512,32]{0,1:T(8,128)S(1)} collective-permute-done((f32[512,32]{0,1:T(8,128)S(1)}, f32[512,32]{0,1:T(8,128)S(1)}, u32[]{:S(2)}, u32[]{:S(2)}) %collective-permute-start.1) | collective-permute-done | bytes 65568 | tf_op jit(solution)/shard_map/ppermute | solution.py:104
  157.8 1.6 collective-permute-start.2
  159.4 4.2 %collective-permute-done.2 = f32[512,32]{0,1:T(8,128)S(1)} collective-permute-done((f32[512,32]{0,1:T(8,128)S(1)}, f32[512,32]{0,1:T(8,128)S(1)}, u32[]{:S(2)}, u32[]{:S(2)}) %collective-permute-start.2) | collective-permute-done | bytes 65568 | tf_op jit(solution)/shard_map/ppermute | solution.py:104
  163.7 2.4 collective-permute-start.3
  166.1 5.9 %collective-permute-done.3 = f32[512,32]{0,1:T(8,128)S(1)} collective-permute-done((f32[512,32]{0,1:T(8,128)S(1)}, f32[512,32]{0,1:T(8,128)S(1)}, u32[]{:S(2)}, u32[]{:S(2)}) %collective-permute-start.3) | collective-permute-done | bytes 65568 | tf_op jit(solution)/shard_map/ppermute | solution.py:104
  171.9 0.1 broadcast_in_dim.5
  172.1 17.8 %all_to_all.16 = f32[16,32,512]{2,1,0:T(8,128)} all-to-all(f32[16,32,512]{2,1,0:T(8,128)S(1)} %broadcast_in_dim.5), channel_id=1, replica_groups=mesh['row'=16,'col'=16] {'col'}, dimensions={0} | all-to-all | bytes 2097152 | tf_op jit(solution)/shard_map/all_to_all | solution.py:96
  189.8 0.0 copy-done
  189.8 49.2 %shard_map.41 = (f32[512,512]{1,0:T(8,128)}, f32[16,512]{1,0:T(8,128)}) custom-call(f32[512,512]{1,0:T(8,128)} %bitcast.8, f32[16,512]{1,0:T(8,128)} %copy-done), custom_call_target="tpu_custom_call" | custom-call | tf_op jit(solution)/shard_map/pallas_call | solution.py:67
  (5 shorter events, 0.1 us)
Async XLA Ops:
  7.2 101.0 %all-gather.2.cloned.1.call-start = ((), (), s32[]{:S(2)}) async-start(), calls=%async_computation.3 | async-start | bytes 17825792 | tf_op jit(solution)/shard_map/all_gather | solution.py:84
  136.3 53.5 %copy-start = (f32[16,512]{1,0:T(8,128)}, f32[16,512]{1,0:T(8,128)S(1)}, u32[]{:S(2)}) copy-start(f32[16,512]{1,0:T(8,128)S(1)} %reduce_sum.9.e_ref) | copy-start | bytes 98308
  137.2 14.4 %all-to-all-start.1 = ((f32[16,16,512]{2,1,0:T(8,128)}), f32[16,16,512]{2,1,0:T(8,128)S(1)}, u32[]{:S(2)}, u32[]{:S(2)}) async-start(f32[16,16,512]{2,1,0:T(8,128)} %broadcast_in_dim.4), calls=%async_computation.1 | async-start | bytes 1048576 | tf_op jit(solution)/shard_map/all_to_all | solution.py:96
  152.1 1.3 collective-permute-start
  153.4 4.4 %collective-permute-start.1 = (f32[512,32]{0,1:T(8,128)S(1)}, f32[512,32]{0,1:T(8,128)S(1)}, u32[]{:S(2)}, u32[]{:S(2)}) collective-permute-start(f32[512,32]{0,1:T(8,128)S(1)} %add.16), channel_id=1, source_target_pairs={{0,32},{16,48},{32,0},{48,16},{64,96},{80,112},{96,64},{112,80},{1... | collective-permute-start | bytes 196616 | tf_op jit(solution)/shard_map/ppermute | solution.py:104
  157.8 5.8 %collective-permute-start.2 = (f32[512,32]{0,1:T(8,128)S(1)}, f32[512,32]{0,1:T(8,128)S(1)}, u32[]{:S(2)}, u32[]{:S(2)}) collective-permute-start(f32[512,32]{0,1:T(8,128)S(1)} %add.17), channel_id=1, source_target_pairs={{0,64},{16,80},{32,96},{48,112},{64,0},{80,16},{96,32},{112,48},{1... | collective-permute-start | bytes 196616 | tf_op jit(solution)/shard_map/ppermute | solution.py:104
  163.7 8.3 %collective-permute-start.3 = (f32[512,32]{0,1:T(8,128)S(1)}, f32[512,32]{0,1:T(8,128)S(1)}, u32[]{:S(2)}, u32[]{:S(2)}) collective-permute-start(f32[512,32]{0,1:T(8,128)S(1)} %add.18), channel_id=1, source_target_pairs={{0,128},{16,144},{32,160},{48,176},{64,192},{80,208},{96,224},{112... | collective-permute-start | bytes 196616 | tf_op jit(solution)/shard_map/ppermute | solution.py:104
Sparse Core Ops, SparseCore 0:
  9.8 98.2 all-gather.1
